TPU v7x, 32 devices: a whole 2x2x4 slice. The times are simulated.
32 devices in a mesh: group: 2 (over y), cell: 8 (over z, x), head: 2 (over core).
Axes of the slice: x: 2, y: 2, z: 4, core: 2. Of those that a mesh axis runs over, the one named last changes fastest.
Arguments:
- latents: bfloat16 [4096, 1024], P(('group', 'cell')), parts along dimension 0, may hold values from -6.2 to 6.2
- cells: bfloat16 [16384, 1024], P(('group', 'cell')), parts along dimension 0, may hold values from -6 to 6
- w_query: bfloat16 [1024, 1024], P(None, 'head'), may hold values from -1.53125 to 1.53125
- w_key: bfloat16 [1024, 1024], P(None, 'head'), may hold values from -0.134375 to 0.134375
- w_value: bfloat16 [1024, 1024], P(None, 'head'), may hold values from -0.1875 to 0.1875
- w_out: bfloat16 [1024, 1024], replicated, may hold values from -0.1875 to 0.1875
- w_up: bfloat16 [1024, 4096], P(None, ('cell', 'head')), may hold values from -0.1875 to 0.1875
- w_down: bfloat16 [4096, 1024], P(('cell', 'head')), may hold values from -0.09375 to 0.09375
Outputs:
- prototypes: bfloat16 [4096, 1024], P(('group', 'cell', 'head')), parts along dimension 0
There are 2 independent parts, one for each index of `group`. A program takes and returns all parts, laid end to end along the dimension named above; an argument that names none is the same for every part. Nothing has to cross between parts.
All inputs are finite; a program needn't handle non-finite values.
Results may differ from a plain program's by a relative error of at most 0.015.
Values may be sent and summed in bfloat16 or wider, within the bound.
No kernel may reach another device: no remote copies, remote signals or barrier semaphores. Data moves between devices by JAX's collectives and lax.ppermute only.
A program may use at most 128 MiB of HBM per device.

v0:
```python
import jax
import jax.numpy as jnp
from jax import lax
from jax.sharding import PartitionSpec as P

HEAD_DIM = 64


def pair_slice(matrix, pair_index, pair_width):
    return lax.dynamic_slice_in_dim(matrix, pair_index * pair_width, pair_width, 1)


def body(latents, cells, w_query, w_key, w_value, w_out, w_up, w_down):
    factor = HEAD_DIM ** (-0.5)
    pair_width = 2 * HEAD_DIM
    key_rows = jnp.dot(cells, w_key, preferred_element_type=jnp.float32).astype(jnp.bfloat16)
    value_rows = jnp.dot(cells, w_value, preferred_element_type=jnp.float32).astype(jnp.bfloat16)
    local_queries = jnp.dot(latents, w_query, preferred_element_type=jnp.float32).astype(
        jnp.bfloat16
    )
    queries = lax.all_gather(local_queries, "cell", axis=0, tiled=True)
    latent_count = queries.shape[0]
    cell_count = cells.shape[0]
    pair_count = w_query.shape[1] // pair_width
    pair_ids = jnp.arange(pair_count, dtype=jnp.int32)

    def pair_partial(pair_index):
        query_pair = pair_slice(queries, pair_index, pair_width).reshape(latent_count, 2, HEAD_DIM)
        key_pair = pair_slice(key_rows, pair_index, pair_width).reshape(cell_count, 2, HEAD_DIM)
        scores = (
            jnp.einsum("lhd,chd->hlc", query_pair, key_pair, preferred_element_type=jnp.float32)
            * factor
        )
        block_max = jnp.max(scores, axis=2)
        weights = jnp.exp(scores - block_max[:, :, None])
        totals = jnp.sum(weights, axis=2)
        value_pair = pair_slice(value_rows, pair_index, pair_width).reshape(cell_count, 2, HEAD_DIM)
        summed = jnp.einsum(
            "hlc,chd->lhd",
            weights.astype(jnp.bfloat16),
            value_pair,
            preferred_element_type=jnp.float32,
        )
        return (summed.reshape(latent_count, pair_width), totals, block_max)

    partial_out, partial_tot, block_max = lax.map(pair_partial, pair_ids)
    maxima = lax.pmax(block_max.astype(jnp.bfloat16), "cell").astype(block_max.dtype)
    shrink = jnp.exp(block_max - maxima)
    scaled_out = (
        partial_out.reshape(pair_count, latent_count, 2, HEAD_DIM)
        * jnp.transpose(shrink, (0, 2, 1))[:, :, :, None]
    )
    scaled_out = scaled_out.reshape(pair_count, latent_count, pair_width)
    scaled_tot = partial_tot * shrink
    rows_cell = latent_count // lax.axis_size("cell")
    summed_out, summed_tot = lax.psum((scaled_out, scaled_tot), "cell")
    first_row = lax.axis_index("cell") * rows_cell
    summed_out = lax.dynamic_slice_in_dim(summed_out, first_row, rows_cell, 1)
    summed_tot = lax.dynamic_slice_in_dim(summed_tot, first_row, rows_cell, 2)
    ratios = (
        summed_out.reshape(pair_count, rows_cell, 2, HEAD_DIM)
        / jnp.transpose(summed_tot, (0, 2, 1))[:, :, :, None]
    )
    attended = (
        jnp.transpose(ratios, (1, 0, 2, 3))
        .reshape(rows_cell, pair_count * pair_width)
        .astype(jnp.bfloat16)
    )
    half_rows = rows_cell // lax.axis_size("head")
    own_latents = lax.dynamic_slice_in_dim(
        latents, lax.axis_index("head") * half_rows, half_rows, 0
    )
    all_heads = lax.all_to_all(attended, "head", split_axis=0, concat_axis=1, tiled=True)
    projected = jnp.dot(all_heads, w_out, preferred_element_type=jnp.float32)
    updated = (own_latents.astype(jnp.float32) + projected).astype(jnp.bfloat16)
    widened = updated.astype(jnp.float32)
    normed = (
        widened * lax.rsqrt(jnp.mean(widened * widened, axis=1, keepdims=True) + 1e-05)
    ).astype(jnp.bfloat16)
    hidden = jax.nn.gelu(
        jnp.dot(
            normed,
            lax.all_gather(w_up, ("cell", "head"), axis=1, tiled=True),
            preferred_element_type=jnp.float32,
        ),
        approximate=True,
    ).astype(jnp.bfloat16)
    mlp_out = jnp.dot(
        hidden,
        lax.all_gather(w_down, ("cell", "head"), axis=0, tiled=True),
        preferred_element_type=jnp.float32,
    )
    return (widened + mlp_out).astype(jnp.bfloat16)


def solution(mesh):
    return jax.shard_map(
        body,
        mesh=mesh,
        in_specs=(
            P(("group", "cell"), None),
            P(("group", "cell"), None),
            P(None, "head"),
            P(None, "head"),
            P(None, "head"),
            P(),
            P(None, ("cell", "head")),
            P(("cell", "head"), None),
        ),
        out_specs=P(("group", "cell", "head"), None),
        check_vma=False,
    )
```

profile of v0, /device:TPU:0, one launch (start us, length us, event | category | flops | bytes accessed | tf_op | source)
XLA Modules:
  0.0 472.5 jit_solution(204552376012297400)
XLA Ops:
  7.4 2.7 convolution_convert_fusion.2
  10.2 3.6 convolution_convert_fusion
  13.7 2.2 convolution_convert_fusion.1
  16.0 46.2 %all-gather.4.cloned.1.call-done = bf16[2048,512]{1,0:T(8,128)(2,1)} async-done(((bf16[256,512]{1,0:T(8,128)(2,1)}), bf16[2048,512]{1,0:T(8,128)(2,1)}) %all-gather.4.cloned.1.call-update) | async-done | bytes 2097168 | tf_op jit(solution)/shard_map/all_gather | solution.py:21
  62.1 119.4 %while.14 = (s32[]{:T(128)}, f32[4,2048,128]{1,2,0:T(8,128)}, f32[4,2,2048]{2,1,0:T(2,128)S(1)}, f32[4,2,2048]{2,1,0:T(2,128)S(1)}, s32[4]{0:T(128)S(1)}, /*inde...) while((s32[]{:T(128)}, f32[4,2048,128]{1,2,0:T(8,128)}, ...), condition=%wide.region_3.4_spmd, body=%wide.region_0.3_spmd.sunk | while | flops 1107288064 | bytes 58852028 | solution.py:46
  62.1 0.6 dynamic_slice.38
  63.4 1.1 constant_dynamic-slice_fusion.8
  64.7 1.0 constant_dynamic-slice_fusion.9
  65.8 8.1 %multiply_reduce_fusion.3 = (f32[2,2048]{1,0:T(2,128)S(1)}, f32[2,2048,1024]{1,2,0:T(8,128)}) fusion(bf16[2048,2,64]{0,2,1:T(8,128)(2,1)S(1)} %bitcast.59, bf16[1024,2,64]{0,2,1:T(8,128)(2,1)S(1)} %bitcast.60), kind=kOutput, calls=%fused_computation.1.clone.1 | convolution fusion | flops 545255424 | bytes 17580032 | tf_op jit(solution)/shard_map/while/body/eval_jaxpr/lhd,chd->hlc/dot_general | solution.py:31
  73.9 8.5 %fusion.55 = f32[2,2048]{1,0:T(2,128)S(1)} fusion(f32[2,2048,1024]{1,2,0:T(8,128)} %get-tuple-element.163, f32[2,2048]{1,0:T(2,128)S(1)} %get-tuple-element.164), kind=kLoop, calls=%fused_computation.2.clone.1 | loop fusion | flops 12578816 | bytes 16809984 | tf_op jit(solution)/shard_map/while/body/eval_jaxpr/reduce_sum | solution.py:36
  82.5 1.0 constant_dynamic-slice_fusion.7
  83.6 7.3 %fusion.54 = f32[2,64,2048]{2,1,0:T(8,128)S(1)} fusion(bf16[1024,2,64]{0,2,1:T(8,128)(2,1)S(1)} %bitcast.61, f32[2,2048,1024]{1,2,0:T(8,128)} %get-tuple-element.163, f32[2,2048]{1,0:T(2,128)S(1)} %get-tuple-element.164), kind=kOutput, calls=%fused_computation.4.clone.1 | convolution fusion | flops 549453824 | bytes 18104320 | tf_op jit(solution)/shard_map/while/body/eval_jaxpr/hlc,chd->lhd/dot_general | solution.py:38
  90.9 1.1 constant_dynamic-update-slice_fusion.2
  92.0 0.6 dynamic_slice.38
  93.2 1.1 constant_dynamic-slice_fusion.8
  94.5 1.0 constant_dynamic-slice_fusion.9
  95.6 8.1 %multiply_reduce_fusion.3 = (f32[2,2048]{1,0:T(2,128)S(1)}, f32[2,2048,1024]{1,2,0:T(8,128)}) fusion(bf16[2048,2,64]{0,2,1:T(8,128)(2,1)S(1)} %bitcast.59, bf16[1024,2,64]{0,2,1:T(8,128)(2,1)S(1)} %bitcast.60), kind=kOutput, calls=%fused_computation.1.clone.1 | convolution fusion | flops 545255424 | bytes 17580032 | tf_op jit(solution)/shard_map/while/body/eval_jaxpr/lhd,chd->hlc/dot_general | solution.py:31
  103.8 8.5 %fusion.55 = f32[2,2048]{1,0:T(2,128)S(1)} fusion(f32[2,2048,1024]{1,2,0:T(8,128)} %get-tuple-element.163, f32[2,2048]{1,0:T(2,128)S(1)} %get-tuple-element.164), kind=kLoop, calls=%fused_computation.2.clone.1 | loop fusion | flops 12578816 | bytes 16809984 | tf_op jit(solution)/shard_map/while/body/eval_jaxpr/reduce_sum | solution.py:36
  112.3 1.0 constant_dynamic-slice_fusion.7
  113.4 7.3 %fusion.54 = f32[2,64,2048]{2,1,0:T(8,128)S(1)} fusion(bf16[1024,2,64]{0,2,1:T(8,128)(2,1)S(1)} %bitcast.61, f32[2,2048,1024]{1,2,0:T(8,128)} %get-tuple-element.163, f32[2,2048]{1,0:T(2,128)S(1)} %get-tuple-element.164), kind=kOutput, calls=%fused_computation.4.clone.1 | convolution fusion | flops 549453824 | bytes 18104320 | tf_op jit(solution)/shard_map/while/body/eval_jaxpr/hlc,chd->lhd/dot_general | solution.py:38
  120.7 1.1 constant_dynamic-update-slice_fusion.2
  121.9 0.6 dynamic_slice.38
  123.1 1.1 constant_dynamic-slice_fusion.8
  124.4 1.0 constant_dynamic-slice_fusion.9
  125.5 8.1 %multiply_reduce_fusion.3 = (f32[2,2048]{1,0:T(2,128)S(1)}, f32[2,2048,1024]{1,2,0:T(8,128)}) fusion(bf16[2048,2,64]{0,2,1:T(8,128)(2,1)S(1)} %bitcast.59, bf16[1024,2,64]{0,2,1:T(8,128)(2,1)S(1)} %bitcast.60), kind=kOutput, calls=%fused_computation.1.clone.1 | convolution fusion | flops 545255424 | bytes 17580032 | tf_op jit(solution)/shard_map/while/body/eval_jaxpr/lhd,chd->hlc/dot_general | solution.py:31
  133.6 8.5 %fusion.55 = f32[2,2048]{1,0:T(2,128)S(1)} fusion(f32[2,2048,1024]{1,2,0:T(8,128)} %get-tuple-element.163, f32[2,2048]{1,0:T(2,128)S(1)} %get-tuple-element.164), kind=kLoop, calls=%fused_computation.2.clone.1 | loop fusion | flops 12578816 | bytes 16809984 | tf_op jit(solution)/shard_map/while/body/eval_jaxpr/reduce_sum | solution.py:36
  142.2 1.0 constant_dynamic-slice_fusion.7
  143.3 7.3 %fusion.54 = f32[2,64,2048]{2,1,0:T(8,128)S(1)} fusion(bf16[1024,2,64]{0,2,1:T(8,128)(2,1)S(1)} %bitcast.61, f32[2,2048,1024]{1,2,0:T(8,128)} %get-tuple-element.163, f32[2,2048]{1,0:T(2,128)S(1)} %get-tuple-element.164), kind=kOutput, calls=%fused_computation.4.clone.1 | convolution fusion | flops 549453824 | bytes 18104320 | tf_op jit(solution)/shard_map/while/body/eval_jaxpr/hlc,chd->lhd/dot_general | solution.py:38
  150.6 1.1 constant_dynamic-update-slice_fusion.2
  151.7 0.6 dynamic_slice.38
  152.9 1.1 constant_dynamic-slice_fusion.8
  154.2 1.0 constant_dynamic-slice_fusion.9
  155.4 8.1 %multiply_reduce_fusion.3 = (f32[2,2048]{1,0:T(2,128)S(1)}, f32[2,2048,1024]{1,2,0:T(8,128)}) fusion(bf16[2048,2,64]{0,2,1:T(8,128)(2,1)S(1)} %bitcast.59, bf16[1024,2,64]{0,2,1:T(8,128)(2,1)S(1)} %bitcast.60), kind=kOutput, calls=%fused_computation.1.clone.1 | convolution fusion | flops 545255424 | bytes 17580032 | tf_op jit(solution)/shard_map/while/body/eval_jaxpr/lhd,chd->hlc/dot_general | solution.py:31
  163.5 8.5 %fusion.55 = f32[2,2048]{1,0:T(2,128)S(1)} fusion(f32[2,2048,1024]{1,2,0:T(8,128)} %get-tuple-element.163, f32[2,2048]{1,0:T(2,128)S(1)} %get-tuple-element.164), kind=kLoop, calls=%fused_computation.2.clone.1 | loop fusion | flops 12578816 | bytes 16809984 | tf_op jit(solution)/shard_map/while/body/eval_jaxpr/reduce_sum | solution.py:36
  172.0 1.0 constant_dynamic-slice_fusion.7
  173.2 7.3 %fusion.54 = f32[2,64,2048]{2,1,0:T(8,128)S(1)} fusion(bf16[1024,2,64]{0,2,1:T(8,128)(2,1)S(1)} %bitcast.61, f32[2,2048,1024]{1,2,0:T(8,128)} %get-tuple-element.163, f32[2,2048]{1,0:T(2,128)S(1)} %get-tuple-element.164), kind=kOutput, calls=%fused_computation.4.clone.1 | convolution fusion | flops 549453824 | bytes 18104320 | tf_op jit(solution)/shard_map/while/body/eval_jaxpr/hlc,chd->lhd/dot_general | solution.py:38
  180.5 1.1 constant_dynamic-update-slice_fusion.2
  181.6 34.7 %pmax.7 = bf16[4,2,2048]{2,1,0:T(2,128)(2,1)S(1)} all-reduce(bf16[4,2,2048]{2,1,0:T(2,128)(2,1)S(1)} %convert_element_type.50), channel_id=1, replica_groups=mesh['group'=2,'cell'=8,'head'=2] {'cell'}, use_global_device_ids=true, to_apply=%region_4.5 | all-reduce | flops 16384 | bytes 65536 | tf_op jit(solution)/shard_map/pmax | solution.py:47
  216.3 0.7 fusion.25
  217.0 4.8 %bitcast_multiply_fusion = f32[4,2048,128]{1,2,0:T(8,128)} fusion(f32[4,2048,128]{1,2,0:T(8,128)} %get-tuple-element.49, f32[4,2048,2]{1,2,0:T(2,128)S(1)} %get-tuple-element.107), kind=kLoop, calls=%fused_computation.12 | loop fusion | flops 1048576 | bytes 8454144 | tf_op jit(solution)/shard_map/mul | solution.py:50
  222.5 0.5 all-gather.8.cloned.1.call-update
  223.0 221.5 %all-reduce.3.cloned.1.call-done = (f32[4,2048,128]{1,2,0:T(8,128)}, f32[4,2,2048]{2,1,0:T(2,128)}) async-done(((f32[4,2048,128]{1,2,0:T(8,128)}, f32[4,2,2048]{2,1,0:T(2,128)}), (f32[4,2048,128]{1,2,0:T(8,128)}, f32[4,2,2048]{2,1,0:T(2,128)})) %all-reduce.3.cloned.1.call-update) | async-done | bytes 4259856 | tf_op jit(solution)/shard_map/psum | solution.py:56
  444.5 0.7 dynamic-slice_bitcast_fusion
  445.2 1.1 constant_dynamic-slice_fusion.3
  446.5 3.9 all_to_all.16
  450.4 2.1 multiply_reduce_fusion.1
  452.6 3.3 all-gather.8.cloned.1.call-done
  455.9 9.2 %fusion.13 = bf16[128,1024]{1,0:T(8,128)(2,1)} fusion(f32[128,1024]{1,0:T(8,128)S(1)} %get-tuple-element.109, bf16[4096,1024]{1,0:T(8,128)(2,1)} %all-gather.8.cloned.1.call-done, bf16[1024,4096]{1,0:T(8,128)(2,1)} %all-gather.6.cloned.1.call-done, f32[128]{0:T(128)S(1)} %add_rsqrt_fusion), kind=kOutput, calls=%fused_computation.26 | convolution fusion | flops 2152726528 | bytes 17564160 | tf_op jit(solution)/shard_map/dot_general | solution.py:88
  (39 shorter events, 3.0 us)
Async XLA Ops:
  7.4 2.8 copy-start
  7.4 54.8 %all-gather.4.cloned.1.call-start = ((), (), s32[]{:S(2)}) async-start(), calls=%async_computation.1 | async-start | bytes 2359296 | tf_op jit(solution)/shard_map/all_gather | solution.py:21
  10.1 434.4 %all-reduce.3.cloned.1.call-start = ((), (), s32[]{:S(2)}) async-start(), calls=%async_computation.4 | async-start | bytes 8519680 | tf_op jit(solution)/shard_map/psum | solution.py:56
  10.2 3.6 copy-start.2
  221.8 228.6 %copy-start.1 = (bf16[256,1024]{1,0:T(8,128)(2,1)S(1)}, bf16[256,1024]{1,0:T(8,128)(2,1)}, u32[]{:S(2)}) copy-start(bf16[256,1024]{1,0:T(8,128)(2,1)} %param.10) | copy-start | bytes 1572868
  221.9 230.7 %all-gather.6.cloned.1.call-start = ((), (), s32[]{:S(2)}) async-start(), calls=%async_computation.2 | async-start | bytes 8912896 | tf_op jit(solution)/shard_map/all_gather | solution.py:83
  222.4 233.5 %all-gather.8.cloned.1.call-start = ((), (), s32[]{:S(2)}) async-start(), calls=%async_computation.3 | async-start | bytes 8912896 | tf_op jit(solution)/shard_map/all_gather | solution.py:90
Sparse Core Ops, SparseCore 0:
  10.3 51.7 all-gather.3
  222.0 222.4 all-reduce.2
Sparse Core Ops, SparseCore 1:
  224.5 118.9 all-gather.5
  345.5 110.4 all-gather.7
where the time goes:
time: 474 us; the launch traced here: 473 us
  waiting for transfers between devices  272 us (57%)
  matrix products  81.5 us (17%)
  other arithmetic  39.7 us (8%)
  blocking collectives  38.7 us (8%)
  local copies, waits for them, and re-layouts  22.8 us (5%)
  between operations  14.9 us (3%)
    psum x1, waiting for transfers between devices, body(): summed_out, summed_tot = lax.psum((scaled_out, scaled_tot), 'cell')  221 us
    all_gather x1, waiting for transfers between devices, body(): queries = lax.all_gather(local_queries, 'cell', axis=0, tiled=True)  46.2 us
    pmax x1, blocking collectives, body(): lax.pmax(block_max.astype(jnp.bfloat16), 'cell').astype(block_max.dtype)  34.7 us
    reduce_sum x4, other arithmetic, pair_partial(): totals = jnp.sum(weights, axis=2)  34 us
    dot_general x4, matrix products, pair_partial(): jnp.einsum('lhd,chd->hlc', query_pair, key_pair, preferred_element_type=j...  32.5 us
    dot_general x4, matrix products, pair_partial(): jnp.einsum('hlc,chd->lhd', weights.astype(jnp.bfloat16), value_pair, pref...  29.2 us
    dynamic_slice x24, local copies, waits for them, and re-layouts, pair_slice(): lax.dynamic_slice_in_dim(matrix, pair_index * pair_width, pair_width, 1)  14.1 us
  transfers between devices with their start and end apart: 4, of which 3 were waited for; matrix products, arithmetic and copies ran while one was open for 2% of the time, Pallas kernels for 0%

commit v1 on v0

v1 whole, which is shorter than its diff:
```python
import functools

import jax
import jax.numpy as jnp
from jax import lax
from jax.experimental import pallas as pl
from jax.experimental.pallas import tpu as pltpu
from jax.sharding import PartitionSpec as P

HEAD_DIM = 64
LAT_TILE = 512


def attention_kernel(q_ref, k_ref, vt_ref, o_ref, ml_ref):
    factor = HEAD_DIM ** (-0.5)
    for j in range(2):
        cols = slice(j * HEAD_DIM, (j + 1) * HEAD_DIM)
        q = q_ref[:, cols]
        k = k_ref[:, cols]
        scores = (
            lax.dot_general(k, q, (((1,), (1,)), ((), ())), preferred_element_type=jnp.float32)
            * factor
        )
        block_max = jnp.max(scores, axis=0, keepdims=True)
        weights = jnp.exp(scores - block_max)
        block_tot = jnp.sum(weights, axis=0, keepdims=True)
        summed = jnp.dot(
            vt_ref[cols, :], weights.astype(jnp.bfloat16), preferred_element_type=jnp.float32
        )
        o_ref[cols, :] = summed
        ml_ref[0, j : j + 1, :] = block_max
        ml_ref[1, j : j + 1, :] = block_tot


def block_attention(queries, key_rows, value_t):
    lat, width = queries.shape
    cells = key_rows.shape[0]
    pairs = width // (2 * HEAD_DIM)
    tile = min(LAT_TILE, lat)
    return pl.pallas_call(
        attention_kernel,
        grid=(pairs, lat // tile),
        in_specs=[
            pl.BlockSpec((tile, 2 * HEAD_DIM), lambda p, i: (i, p)),
            pl.BlockSpec((cells, 2 * HEAD_DIM), lambda p, i: (0, p)),
            pl.BlockSpec((2 * HEAD_DIM, cells), lambda p, i: (p, 0)),
        ],
        out_specs=[
            pl.BlockSpec((2 * HEAD_DIM, tile), lambda p, i: (p, i)),
            pl.BlockSpec((2, None, 2, tile), lambda p, i: (0, p, 0, i)),
        ],
        out_shape=[
            jax.ShapeDtypeStruct((width, lat), jnp.float32),
            jax.ShapeDtypeStruct((2, pairs, 2, lat), jnp.float32),
        ],
    )(queries, key_rows, value_t)


def body(latents, cells, w_query, w_key, w_value, w_out, w_up, w_down):
    key_rows = jnp.dot(cells, w_key, preferred_element_type=jnp.float32).astype(jnp.bfloat16)
    value_t = jnp.dot(cells, w_value, preferred_element_type=jnp.float32).astype(jnp.bfloat16).T
    local_queries = jnp.dot(latents, w_query, preferred_element_type=jnp.float32).astype(
        jnp.bfloat16
    )
    queries = lax.all_gather(local_queries, "cell", axis=0, tiled=True)
    lat, width = queries.shape
    heads_local = width // HEAD_DIM
    n_cell = lax.axis_size("cell")
    n_head = lax.axis_size("head")
    owners = n_cell * n_head
    rows = lat // owners

    sums_t, ml = block_attention(queries, key_rows, value_t)
    ml = ml.reshape(2 * heads_local, lat)
    sums_recv = lax.all_to_all(
        sums_t.astype(jnp.bfloat16), ("cell", "head"), split_axis=1, concat_axis=0, tiled=True
    )
    ml_recv = lax.all_to_all(ml, ("cell", "head"), split_axis=1, concat_axis=0, tiled=True)
    sums_recv = sums_recv.reshape(n_cell, n_head, heads_local, HEAD_DIM, rows).astype(jnp.float32)
    ml_recv = ml_recv.reshape(n_cell, n_head, 2, heads_local, rows)
    block_max = ml_recv[:, :, 0]
    block_tot = ml_recv[:, :, 1]
    maxima = jnp.max(block_max, axis=0)
    shrink = jnp.exp(block_max - maxima[None])
    totals = jnp.sum(shrink * block_tot, axis=0)
    summed = jnp.sum(shrink[:, :, :, None, :] * sums_recv, axis=0)
    attended_t = summed / totals[:, :, None, :]
    attended = attended_t.reshape(n_head * width, rows).T.astype(jnp.bfloat16)

    own_index = lax.axis_index("cell") * n_head + lax.axis_index("head")
    local_rows = latents.shape[0]
    own_latents = lax.dynamic_slice_in_dim(
        latents, (own_index % (local_rows // rows)) * rows, rows, 0
    )
    projected = jnp.dot(attended, w_out, preferred_element_type=jnp.float32)
    updated = (own_latents.astype(jnp.float32) + projected).astype(jnp.bfloat16)
    widened = updated.astype(jnp.float32)
    normed = (
        widened * lax.rsqrt(jnp.mean(widened * widened, axis=1, keepdims=True) + 1e-05)
    ).astype(jnp.bfloat16)
    hidden = jax.nn.gelu(
        jnp.dot(
            normed,
            lax.all_gather(w_up, ("cell", "head"), axis=1, tiled=True),
            preferred_element_type=jnp.float32,
        ),
        approximate=True,
    ).astype(jnp.bfloat16)
    mlp_out = jnp.dot(
        hidden,
        lax.all_gather(w_down, ("cell", "head"), axis=0, tiled=True),
        preferred_element_type=jnp.float32,
    )
    return (widened + mlp_out).astype(jnp.bfloat16)


def solution(mesh):
    return jax.shard_map(
        body,
        mesh=mesh,
        in_specs=(
            P(("group", "cell"), None),
            P(("group", "cell"), None),
            P(None, "head"),
            P(None, "head"),
            P(None, "head"),
            P(),
            P(None, ("cell", "head")),
            P(("cell", "head"), None),
        ),
        out_specs=P(("group", "cell", "head"), None),
        check_vma=False,
    )
```

time: 474 us -> 265 us (0.56)
  waiting for transfers between devices: 272 us -> 178 us
  matrix products: 81.5 us -> 17 us
  blocking collectives: 38.7 us -> 0 us
  Pallas kernels: 0 us -> 35.2 us
  other arithmetic: 39.7 us -> 10.9 us
  local copies, waits for them, and re-layouts: 22.8 us -> 1.8 us
  starting transfers between devices: 0.13 us -> 8.2 us
    psum x1 -> x0, waiting for transfers between devices: 221 us -> none  [body(): summed_out, summed_tot = lax.psum((scaled_out, scaled_tot), 'cell')]
    all_to_all x0 -> x2, waiting for transfers between devices: none -> 63.9 us  [the longest x1 57.5 us: body(): lax.all_to_all(sums_t.astype(jnp.bfloat16), ('cell', 'head'), split_axis=...]
    dot_general x9 -> x1, matrix products: 63.9 us -> 0.55 us  [body(): projected = jnp.dot(attended, w_out, preferred_element_type=jnp.float32)]
    all_gather x1, waiting for transfers between devices: 3.33 us -> 66.5 us  [body(): lax.all_gather(w_down, ('cell', 'head'), axis=0, tiled=True)]
    pallas_call x0 -> x1, Pallas kernels: none -> 35.2 us  [block_attention(): pl.pallas_call(attention_kernel, grid=(pairs, lat // tile), in_specs=[pl....]
    pmax x1 -> x0, blocking collectives: 34.7 us -> none  [body(): lax.pmax(block_max.astype(jnp.bfloat16), 'cell').astype(block_max.dtype)]
    reduce_sum x4 -> x2, other arithmetic: 34 us -> 4.9 us  [the longest x1 4.81 us: body(): summed = jnp.sum(shrink[:, :, :, None, :] * sums_recv, axis=0)]
    dynamic_slice x29 -> x0, local copies, waits for them, and re-layouts: 17.5 us -> none  [the longest x24 14.1 us: pair_slice(): lax.dynamic_slice_in_dim(matrix, pair_index * pair_width, pair_width, 1)]
  transfers between devices with their start and end apart: 4 -> 5, of which waited for: 3 -> 4; matrix products, arithmetic and copies ran while one was open for 2% -> 6% of each run, Pallas kernels for 0% -> 13%
where the time goes in v1:
time: 265 us; the launch traced here: 264 us
  waiting for transfers between devices  178 us (67%)
  Pallas kernels  35.2 us (13%)
  matrix products  17 us (6%)
  between operations  13.3 us (5%)
  other arithmetic  10.9 us (4%)
  starting transfers between devices  8.2 us (3%)
    all_gather x1, waiting for transfers between devices, body(): lax.all_gather(w_down, ('cell', 'head'), axis=0, tiled=True)  66.5 us
    all_to_all x1, waiting for transfers between devices, body(): lax.all_to_all(sums_t.astype(jnp.bfloat16), ('cell', 'head'), split_axis=...  57.5 us
    all_gather x1, waiting for transfers between devices, body(): queries = lax.all_gather(local_queries, 'cell', axis=0, tiled=True)  46 us
    pallas_call x1, Pallas kernels, block_attention(): pl.pallas_call(attention_kernel, grid=(pairs, lat // tile), in_specs=[pl....  35.2 us
    dot_general x1, matrix products, body(): jnp.dot(hidden, lax.all_gather(w_down, ('cell', 'head'), axis=0, tiled=Tr...  9.19 us
    all_to_all x1, waiting for transfers between devices, body(): lax.all_to_all(ml, ('cell', 'head'), split_axis=1, concat_axis=0, tiled=T...  6.44 us
  transfers between devices with their start and end apart: 5, of which 4 were waited for; matrix products, arithmetic and copies ran while one was open for 6% of the time, Pallas kernels for 13%

profile of v1, /device:TPU:0, one launch (start us, length us, event | category | flops | bytes accessed | tf_op | source)
XLA Modules:
  0.0 264.2 jit_solution(12001434170848273564)
XLA Ops:
  6.5 0.0 copy-start
  6.5 0.0 copy-start.3
  6.5 0.0 all-gather.4.cloned.1.call-start
  6.5 2.7 %convolution_convert_fusion.2 = bf16[256,512]{1,0:T(8,128)(2,1)} fusion(bf16[256,1024]{1,0:T(8,128)(2,1)} %param.8, bf16[1024,512]{1,0:T(8,128)(2,1)} %param.10), kind=kOutput, calls=%fused_computation.18 | convolution fusion | flops 268566528 | bytes 1835008 | tf_op jit(solution)/shard_map/dot_general | solution.py:62
  9.2 0.0 all-gather.4.cloned.1.call-update
  9.2 0.0 all-gather.6.cloned.1.call-start
  9.3 0.7 all-gather.6.cloned.1.call-update
  10.0 0.0 all-gather.8.cloned.1.call-start
  10.0 0.7 all-gather.8.cloned.1.call-update
  10.7 0.0 copy-done
  10.7 0.0 copy-done.3
  10.7 0.0 copy-start.4
  10.8 2.3 convolution_convert_fusion.vt_ref
  13.1 0.0 copy-done.4
  13.1 2.2 convolution_convert_fusion.1.k_ref
  15.3 46.0 %all-gather.4.cloned.1.call-done.q_ref = bf16[2048,512]{1,0:T(8,128)(2,1)} async-done(((bf16[256,512]{1,0:T(8,128)(2,1)}), bf16[2048,512]{1,0:T(8,128)(2,1)}) %all-gather.4.cloned.1.call-update) | async-done | bytes 2097168 | tf_op jit(solution)/shard_map/all_gather | solution.py:65
  61.3 35.2 %shard_map.82 = (f32[512,2048]{1,0:T(8,128)}, f32[2,4,2,2048]{3,2,1,0:T(2,128)}) custom-call(bf16[2048,512]{1,0:T(8,128)(2,1)} %all-gather.4.cloned.1.call-done.q_ref, bf16[1024,512]{1,0:T(8,128)(2,1)} %convolution_convert_fusion.1.k_ref, bf16[512,1024]{1,0:T(8,128)(2,1)} %convolution_convert_fusion.vt_ref), custom_call_target="tpu_custom_call" | custom-call | tf_op jit(solution)/shard_map/pallas_call | solution.py:40
  96.5 1.1 all_to_all.22
  97.6 0.7 copy.20
  98.3 3.5 %all-to-all-start = ((f32[16,16,128]{2,0,1:T(8,128)}), f32[16,16,128]{2,0,1:T(8,128)S(1)}, u32[]{:S(2)}, u32[]{:S(2)}) async-start(f32[16,16,128]{2,0,1:T(8,128)} %copy.20), calls=%async_computation | async-start | bytes 262144 | tf_op jit(solution)/shard_map/all_to_all | solution.py:78
  101.8 4.0 %copy_bitcast_fusion = bf16[512,16,128]{2,0,1:T(8,128)(2,1)} fusion(f32[512,2048]{1,0:T(8,128)} %get-tuple-element.8), kind=kLoop, calls=%fused_computation.11 | loop fusion | flops 1048576 | bytes 6291456 | tf_op jit(solution)/shard_map/all_to_all | solution.py:75
  105.8 6.4 %all-to-all-done = f32[16,16,128]{2,0,1:T(8,128)S(1)} async-done(((f32[16,16,128]{2,0,1:T(8,128)}), f32[16,16,128]{2,0,1:T(8,128)S(1)}, u32[]{:S(2)}, u32[]{:S(2)}) %all-to-all-start) | async-done | bytes 131104 | tf_op jit(solution)/shard_map/all_to_all | solution.py:78
  112.2 4.6 %all-to-all-start.1 = ((bf16[512,16,128]{2,0,1:T(8,128)(2,1)}), bf16[512,16,128]{2,0,1:T(8,128)(2,1)}, u32[]{:S(2)}, u32[]{:S(2)}) async-start(bf16[512,16,128]{2,0,1:T(8,128)(2,1)} %copy_bitcast_fusion), calls=%async_computation.1 | async-start | bytes 4194304 | tf_op jit(solution)/shard_map/all_to_all | solution.py:75
  116.9 0.1 fusion.22
  117.0 57.5 %all-to-all-done.1 = bf16[512,16,128]{2,0,1:T(8,128)(2,1)} async-done(((bf16[512,16,128]{2,0,1:T(8,128)(2,1)}), bf16[512,16,128]{2,0,1:T(8,128)(2,1)}, u32[]{:S(2)}, u32[]{:S(2)}) %all-to-all-start.1) | async-done | bytes 2097184 | tf_op jit(solution)/shard_map/all_to_all | solution.py:75
  174.4 2.0 convert_element_type.63
  176.5 0.0 copy-start.1
  176.5 0.0 copy-start.2
  176.5 4.8 %fusion = f32[2,8,64,128]{3,0,2,1:T(2,128)S(1)} fusion(f32[8,2,8,64,128]{4,3,2,1,0:T(8,128)S(1)} %bitcast.35, f32[8,2,8,128]{3,1,0,2:T(2,128)S(1)} %get-tuple-element.10), kind=kLoop, calls=%fused_computation.1 | loop fusion | flops 1966080 | bytes 4784128 | tf_op jit(solution)/shard_map/reduce_sum | solution.py:86
  181.3 0.1 fusion.17
  181.4 0.0 copy-done.1
  181.4 0.0 copy-done.2
  181.4 0.6 multiply_reduce_fusion
  181.9 0.0 all-gather.6.cloned.1.call-done
  182.0 66.5 %all-gather.8.cloned.1.call-done = bf16[4096,1024]{1,0:T(8,128)(2,1)} async-done(((bf16[256,1024]{1,0:T(8,128)(2,1)}), bf16[4096,1024]{1,0:T(8,128)(2,1)}) %all-gather.8.cloned.1.call-update) | async-done | bytes 8388624 | tf_op jit(solution)/shard_map/all_gather | solution.py:111
  248.4 9.2 %fusion.9 = bf16[128,1024]{1,0:T(8,128)(2,1)} fusion(f32[128,1024]{1,0:T(8,128)S(1)} %get-tuple-element.15, bf16[4096,1024]{1,0:T(8,128)(2,1)} %all-gather.8.cloned.1.call-done, bf16[1024,4096]{1,0:T(8,128)(2,1)} %all-gather.6.cloned.1.call-done, f32[128]{0:T(128)S(1)} %add_rsqrt_fusion), kind=kOutput, calls=%fused_computation.17 | convolution fusion | flops 2152726528 | bytes 17564160 | tf_op jit(solution)/shard_map/dot_general | solution.py:109
  (4 shorter events, 0.0 us)
Async XLA Ops:
  6.5 4.2 %copy-start = (bf16[1024,1024]{1,0:T(8,128)(2,1)S(1)}, bf16[1024,1024]{1,0:T(8,128)(2,1)}, u32[]{:S(2)}) copy-start(bf16[1024,1024]{1,0:T(8,128)(2,1)} %param.9) | copy-start | bytes 6291460
  6.5 4.2 %copy-start.3 = (bf16[1024,512]{1,0:T(8,128)(2,1)S(1)}, bf16[1024,512]{1,0:T(8,128)(2,1)}, u32[]{:S(2)}) copy-start(bf16[1024,512]{1,0:T(8,128)(2,1)} %param.12) | copy-start | bytes 3145732
  6.5 54.8 %all-gather.4.cloned.1.call-start = ((), (), s32[]{:S(2)}) async-start(), calls=%async_computation.2 | async-start | bytes 2359296 | tf_op jit(solution)/shard_map/all_gather | solution.py:65
  9.2 172.7 %all-gather.6.cloned.1.call-start = ((), (), s32[]{:S(2)}) async-start(), calls=%async_computation.3 | async-start | bytes 8912896 | tf_op jit(solution)/shard_map/all_gather | solution.py:104
  10.0 238.5 %all-gather.8.cloned.1.call-start = ((), (), s32[]{:S(2)}) async-start(), calls=%async_computation.4 | async-start | bytes 8912896 | tf_op jit(solution)/shard_map/all_gather | solution.py:111
  10.7 2.3 copy-start.4
  98.3 13.9 %all-to-all-start = ((f32[16,16,128]{2,0,1:T(8,128)}), f32[16,16,128]{2,0,1:T(8,128)S(1)}, u32[]{:S(2)}, u32[]{:S(2)}) async-start(f32[16,16,128]{2,0,1:T(8,128)} %copy.20), calls=%async_computation | async-start | bytes 262144 | tf_op jit(solution)/shard_map/all_to_all | solution.py:78
  112.2 62.2 %all-to-all-start.1 = ((bf16[512,16,128]{2,0,1:T(8,128)(2,1)}), bf16[512,16,128]{2,0,1:T(8,128)(2,1)}, u32[]{:S(2)}, u32[]{:S(2)}) async-start(bf16[512,16,128]{2,0,1:T(8,128)(2,1)} %copy_bitcast_fusion), calls=%async_computation.1 | async-start | bytes 4194304 | tf_op jit(solution)/shard_map/all_to_all | solution.py:75
  176.5 4.9 %copy-start.1 = (bf16[1024,1024]{1,0:T(8,128)(2,1)S(1)}, bf16[1024,1024]{1,0:T(8,128)(2,1)}, u32[]{:S(2)}) copy-start(bf16[1024,1024]{1,0:T(8,128)(2,1)} %param.13) | copy-start | bytes 6291460
  176.5 4.9 %copy-start.2 = (bf16[256,1024]{1,0:T(8,128)(2,1)S(1)}, bf16[256,1024]{1,0:T(8,128)(2,1)}, u32[]{:S(2)}) copy-start(bf16[256,1024]{1,0:T(8,128)(2,1)} %param.8) | copy-start | bytes 1572868
Sparse Core Ops, SparseCore 0:
  9.5 51.7 all-gather.3
  63.5 110.1 all-gather.5
  175.8 72.6 all-gather.7

commit v2 on v1

--- a/solution.py
+++ b/solution.py
@@ -98,19 +98,21 @@
     normed = (
         widened * lax.rsqrt(jnp.mean(widened * widened, axis=1, keepdims=True) + 1e-05)
     ).astype(jnp.bfloat16)
+    chip_normed = lax.all_gather(normed, "head", axis=0, tiled=True)
     hidden = jax.nn.gelu(
         jnp.dot(
-            normed,
-            lax.all_gather(w_up, ("cell", "head"), axis=1, tiled=True),
+            chip_normed,
+            lax.all_gather(w_up, "cell", axis=1, tiled=True),
             preferred_element_type=jnp.float32,
         ),
         approximate=True,
     ).astype(jnp.bfloat16)
-    mlp_out = jnp.dot(
+    mlp_part = jnp.dot(
         hidden,
-        lax.all_gather(w_down, ("cell", "head"), axis=0, tiled=True),
+        lax.all_gather(w_down, "cell", axis=0, tiled=True),
         preferred_element_type=jnp.float32,
     )
+    mlp_out = lax.psum_scatter(mlp_part, "head", scatter_dimension=0, tiled=True)
     return (widened + mlp_out).astype(jnp.bfloat16)
 
 

time: 265 us -> 267 us (level)
    reduce_scatter x0 -> x1, waiting for transfers between devices: none -> 7.07 us  [body(): lax.psum_scatter(mlp_part, 'head', scatter_dimension=0, tiled=True)]
    all_gather x2, waiting for transfers between devices: 66.5 us -> 59.5 us  [the longest x1 59.5 us: body(): lax.all_gather(w_down, 'cell', axis=0, tiled=True)]
  transfers between devices with their start and end apart: 5 -> 6, of which waited for: 4 -> 5; matrix products, arithmetic and copies ran while one was open for 6% -> 6% of each run, Pallas kernels for 13% -> 13%
where the time goes in v2:
time: 267 us; the launch traced here: 266 us
  waiting for transfers between devices  178 us (67%)
  Pallas kernels  35.2 us (13%)
  matrix products  14.8 us (6%)
  between operations  13.3 us (5%)
  other arithmetic  12.8 us (5%)
  starting transfers between devices  8.09 us (3%)
    all_gather x1, waiting for transfers between devices, body(): lax.all_gather(w_down, 'cell', axis=0, tiled=True)  59.5 us
    all_to_all x1, waiting for transfers between devices, body(): lax.all_to_all(sums_t.astype(jnp.bfloat16), ('cell', 'head'), split_axis=...  57.5 us
    all_gather x1, waiting for transfers between devices, body(): queries = lax.all_gather(local_queries, 'cell', axis=0, tiled=True)  46 us
    pallas_call x1, Pallas kernels, block_attention(): pl.pallas_call(attention_kernel, grid=(pairs, lat // tile), in_specs=[pl....  35.2 us
    dot_general x1, matrix products, body(): jnp.dot(hidden, lax.all_gather(w_down, 'cell', axis=0, tiled=True), prefe...  7.11 us
    reduce_scatter x1, waiting for transfers between devices, body(): lax.psum_scatter(mlp_part, 'head', scatter_dimension=0, tiled=True)  7.07 us
    all_to_all x1, waiting for transfers between devices, body(): lax.all_to_all(ml, ('cell', 'head'), split_axis=1, concat_axis=0, tiled=T...  6.46 us
  transfers between devices with their start and end apart: 6, of which 5 were waited for; matrix products, arithmetic and copies ran while one was open for 6% of the time, Pallas kernels for 13%

profile of v2, /device:TPU:0, one launch (start us, length us, event | category | flops | bytes accessed | tf_op | source)
XLA Modules:
  0.0 266.1 jit_solution(579856859904633958)
XLA Ops:
  6.5 0.0 copy-start
  6.5 0.0 copy-start.3
  6.5 0.0 all-gather.4.cloned.1.call-start
  6.5 2.7 %convolution_convert_fusion.2 = bf16[256,512]{1,0:T(8,128)(2,1)} fusion(bf16[256,1024]{1,0:T(8,128)(2,1)} %param.8, bf16[1024,512]{1,0:T(8,128)(2,1)} %param.10), kind=kOutput, calls=%fused_computation.16 | convolution fusion | flops 268566528 | bytes 1835008 | tf_op jit(solution)/shard_map/dot_general | solution.py:62
  9.2 0.0 all-gather.4.cloned.1.call-update
  9.2 0.0 all-gather.6.cloned.1.call-start
  9.3 0.7 all-gather.6.cloned.1.call-update
  10.0 0.0 all-gather.8.cloned.1.call-start
  10.0 0.7 all-gather.8.cloned.1.call-update
  10.7 0.0 copy-done
  10.7 0.0 copy-done.3
  10.7 0.0 copy-start.4
  10.8 2.3 convolution_convert_fusion.vt_ref
  13.0 0.0 copy-done.4
  13.0 2.2 convolution_convert_fusion.1.k_ref
  15.3 46.0 %all-gather.4.cloned.1.call-done.q_ref = bf16[2048,512]{1,0:T(8,128)(2,1)} async-done(((bf16[256,512]{1,0:T(8,128)(2,1)}), bf16[2048,512]{1,0:T(8,128)(2,1)}) %all-gather.4.cloned.1.call-update) | async-done | bytes 2097168 | tf_op jit(solution)/shard_map/all_gather | solution.py:65
  61.3 35.2 %shard_map.82 = (f32[512,2048]{1,0:T(8,128)}, f32[2,4,2,2048]{3,2,1,0:T(2,128)}) custom-call(bf16[2048,512]{1,0:T(8,128)(2,1)} %all-gather.4.cloned.1.call-done.q_ref, bf16[1024,512]{1,0:T(8,128)(2,1)} %convolution_convert_fusion.1.k_ref, bf16[512,1024]{1,0:T(8,128)(2,1)} %convolution_convert_fusion.vt_ref), custom_call_target="tpu_custom_call" | custom-call | tf_op jit(solution)/shard_map/pallas_call | solution.py:40
  96.5 1.0 all_to_all.22
  97.5 0.7 copy.20
  98.2 3.5 %all-to-all-start = ((f32[16,16,128]{2,0,1:T(8,128)}), f32[16,16,128]{2,0,1:T(8,128)S(1)}, u32[]{:S(2)}, u32[]{:S(2)}) async-start(f32[16,16,128]{2,0,1:T(8,128)} %copy.20), calls=%async_computation | async-start | bytes 262144 | tf_op jit(solution)/shard_map/all_to_all | solution.py:78
  101.8 3.9 %copy_bitcast_fusion = bf16[512,16,128]{2,0,1:T(8,128)(2,1)} fusion(f32[512,2048]{1,0:T(8,128)} %get-tuple-element.8), kind=kLoop, calls=%fused_computation.11 | loop fusion | flops 1048576 | bytes 6291456 | tf_op jit(solution)/shard_map/all_to_all | solution.py:75
  105.7 6.5 %all-to-all-done = f32[16,16,128]{2,0,1:T(8,128)S(1)} async-done(((f32[16,16,128]{2,0,1:T(8,128)}), f32[16,16,128]{2,0,1:T(8,128)S(1)}, u32[]{:S(2)}, u32[]{:S(2)}) %all-to-all-start) | async-done | bytes 131104 | tf_op jit(solution)/shard_map/all_to_all | solution.py:78
  112.2 4.4 %all-to-all-start.1 = ((bf16[512,16,128]{2,0,1:T(8,128)(2,1)}), bf16[512,16,128]{2,0,1:T(8,128)(2,1)}, u32[]{:S(2)}, u32[]{:S(2)}) async-start(bf16[512,16,128]{2,0,1:T(8,128)(2,1)} %copy_bitcast_fusion), calls=%async_computation.1 | async-start | bytes 4194304 | tf_op jit(solution)/shard_map/all_to_all | solution.py:75
  116.6 0.0 reduce-scatter.2.cloned.1.call-start
  116.7 0.1 fusion.19
  116.8 57.5 %all-to-all-done.1 = bf16[512,16,128]{2,0,1:T(8,128)(2,1)} async-done(((bf16[512,16,128]{2,0,1:T(8,128)(2,1)}), bf16[512,16,128]{2,0,1:T(8,128)(2,1)}, u32[]{:S(2)}, u32[]{:S(2)}) %all-to-all-start.1) | async-done | bytes 2097184 | tf_op jit(solution)/shard_map/all_to_all | solution.py:75
  174.3 2.0 convert_element_type.63
  176.3 0.0 copy-start.1
  176.3 0.0 copy-start.2
  176.3 4.8 %fusion = f32[2,8,64,128]{3,0,2,1:T(2,128)S(1)} fusion(f32[8,2,8,64,128]{4,3,2,1,0:T(8,128)S(1)} %bitcast.36, f32[8,2,8,128]{3,1,0,2:T(2,128)S(1)} %get-tuple-element.10), kind=kLoop, calls=%fused_computation.1 | loop fusion | flops 1966080 | bytes 4784128 | tf_op jit(solution)/shard_map/reduce_sum | solution.py:86
  181.2 0.1 fusion.17
  181.2 0.0 copy-done.1
  181.2 0.0 copy-done.2
  181.3 0.6 multiply_reduce_fusion
  181.8 0.1 multiply_convert_fusion
  181.9 2.2 all_gather.13
  184.1 0.0 all-gather.6.cloned.1.call-done
  184.1 59.5 %all-gather.8.cloned.1.call-done = bf16[2048,1024]{1,0:T(8,128)(2,1)} async-done(((bf16[256,1024]{1,0:T(8,128)(2,1)}), bf16[2048,1024]{1,0:T(8,128)(2,1)}) %all-gather.8.cloned.1.call-update) | async-done | bytes 4194320 | tf_op jit(solution)/shard_map/all_gather | solution.py:112
  243.6 7.1 %fusion.11 = f32[256,1024]{1,0:T(8,128)} fusion(bf16[2048,1024]{1,0:T(8,128)(2,1)} %all-gather.8.cloned.1.call-done, bf16[256,1024]{1,0:T(8,128)(2,1)S(1)} %all_gather.13, bf16[1024,2048]{1,0:T(8,128)(2,1)} %all-gather.6.cloned.1.call-done), kind=kOutput, calls=%fused_computation.19 | convolution fusion | flops 2152202240 | bytes 9961472 | tf_op jit(solution)/shard_map/dot_general | solution.py:110
  250.7 0.0 reduce-scatter.2.cloned.1.call-update
  250.7 7.1 %reduce-scatter.2.cloned.1.call-done = f32[128,1024]{1,0:T(8,128)} async-done(((f32[256,1024]{1,0:T(8,128)}), f32[128,1024]{1,0:T(8,128)}) %reduce-scatter.2.cloned.1.call-update) | async-done | bytes 524304 | tf_op jit(solution)/shard_map/reduce_scatter | solution.py:115
  257.8 1.8 add_convert_fusion
  (4 shorter events, 0.0 us)
Async XLA Ops:
  6.5 4.2 %copy-start = (bf16[1024,1024]{1,0:T(8,128)(2,1)S(1)}, bf16[1024,1024]{1,0:T(8,128)(2,1)}, u32[]{:S(2)}) copy-start(bf16[1024,1024]{1,0:T(8,128)(2,1)} %param.9) | copy-start | bytes 6291460
  6.5 4.2 %copy-start.3 = (bf16[1024,512]{1,0:T(8,128)(2,1)S(1)}, bf16[1024,512]{1,0:T(8,128)(2,1)}, u32[]{:S(2)}) copy-start(bf16[1024,512]{1,0:T(8,128)(2,1)} %param.12) | copy-start | bytes 3145732
  6.5 54.8 %all-gather.4.cloned.1.call-start = ((), (), s32[]{:S(2)}) async-start(), calls=%async_computation.3 | async-start | bytes 2359296 | tf_op jit(solution)/shard_map/all_gather | solution.py:65
  9.2 174.9 %all-gather.6.cloned.1.call-start = ((), (), s32[]{:S(2)}) async-start(), calls=%async_computation.4 | async-start | bytes 4718592 | tf_op jit(solution)/shard_map/all_gather | solution.py:105
  10.0 233.6 %all-gather.8.cloned.1.call-start = ((), (), s32[]{:S(2)}) async-start(), calls=%async_computation.5 | async-start | bytes 4718592 | tf_op jit(solution)/shard_map/all_gather | solution.py:112
  10.7 2.3 copy-start.4
  98.2 13.9 %all-to-all-start = ((f32[16,16,128]{2,0,1:T(8,128)}), f32[16,16,128]{2,0,1:T(8,128)S(1)}, u32[]{:S(2)}, u32[]{:S(2)}) async-start(f32[16,16,128]{2,0,1:T(8,128)} %copy.20), calls=%async_computation | async-start | bytes 262144 | tf_op jit(solution)/shard_map/all_to_all | solution.py:78
  112.2 62.1 %all-to-all-start.1 = ((bf16[512,16,128]{2,0,1:T(8,128)(2,1)}), bf16[512,16,128]{2,0,1:T(8,128)(2,1)}, u32[]{:S(2)}, u32[]{:S(2)}) async-start(bf16[512,16,128]{2,0,1:T(8,128)(2,1)} %copy_bitcast_fusion), calls=%async_computation.1 | async-start | bytes 4194304 | tf_op jit(solution)/shard_map/all_to_all | solution.py:75
  116.6 141.2 %reduce-scatter.2.cloned.1.call-start = ((), (), s32[]{:S(2)}) async-start(), calls=%async_computation.6 | async-start | bytes 1572864 | tf_op jit(solution)/shard_map/reduce_scatter | solution.py:115
  176.3 4.9 %copy-start.1 = (bf16[1024,1024]{1,0:T(8,128)(2,1)S(1)}, bf16[1024,1024]{1,0:T(8,128)(2,1)}, u32[]{:S(2)}) copy-start(bf16[1024,1024]{1,0:T(8,128)(2,1)} %param.13) | copy-start | bytes 6291460
  176.3 4.9 %copy-start.2 = (bf16[256,1024]{1,0:T(8,128)(2,1)S(1)}, bf16[256,1024]{1,0:T(8,128)(2,1)}, u32[]{:S(2)}) copy-start(bf16[256,1024]{1,0:T(8,128)(2,1)} %param.8) | copy-start | bytes 1572868
Sparse Core Ops, SparseCore 0:
  9.5 51.7 all-gather.3
  63.3 106.9 all-gather.5
  172.5 71.0 all-gather.7
  250.8 6.8 reduce-scatter.1

commit v3 on v2

--- a/solution.py
+++ b/solution.py
@@ -62,10 +62,16 @@
     local_queries = jnp.dot(latents, w_query, preferred_element_type=jnp.float32).astype(
         jnp.bfloat16
     )
-    queries = lax.all_gather(local_queries, "cell", axis=0, tiled=True)
+    n_cell = lax.axis_size("cell")
+    queries = lax.all_to_all(
+        jnp.broadcast_to(local_queries[None], (n_cell,) + local_queries.shape),
+        "cell",
+        split_axis=0,
+        concat_axis=0,
+        tiled=True,
+    ).reshape(n_cell * local_queries.shape[0], local_queries.shape[1])
     lat, width = queries.shape
     heads_local = width // HEAD_DIM
-    n_cell = lax.axis_size("cell")
     n_head = lax.axis_size("head")
     owners = n_cell * n_head
     rows = lat // owners
@@ -100,9 +106,10 @@
     ).astype(jnp.bfloat16)
     chip_normed = lax.all_gather(normed, "head", axis=0, tiled=True)
     hidden = jax.nn.gelu(
-        jnp.dot(
+        lax.dot_general(
             chip_normed,
-            lax.all_gather(w_up, "cell", axis=1, tiled=True),
+            lax.all_gather(w_up.T, "cell", axis=0, tiled=True),
+            (((1,), (1,)), ((), ())),
             preferred_element_type=jnp.float32,
         ),
         approximate=True,

time: 267 us -> 263 us (0.985)
  waiting for transfers between devices: 178 us -> 166 us
  starting transfers between devices: 8.09 us -> 15.6 us
    all_to_all x0 -> x1, waiting for transfers between devices: none -> 67.1 us  [body(): lax.all_to_all(jnp.broadcast_to(local_queries[None], (n_cell,) + local_qu...]
    all_gather x1, waiting for transfers between devices: 59.5 us -> 12.3 us  [body(): lax.all_gather(w_down, 'cell', axis=0, tiled=True)]
    all_gather x2 -> x1, waiting for transfers between devices: 46 us -> 0.01 us  [body(): lax.all_gather(w_up.T, 'cell', axis=0, tiled=True)]
    reduce_scatter x1, waiting for transfers between devices: 7.07 us -> 15.9 us  [body(): lax.psum_scatter(mlp_part, 'head', scatter_dimension=0, tiled=True)]
    all_to_all x0 -> x1, starting transfers between devices: none -> 7.41 us  [body(): lax.all_to_all(jnp.broadcast_to(local_queries[None], (n_cell,) + local_qu...]
    all_to_all x1, waiting for transfers between devices: 57.5 us -> 63 us  [body(): lax.all_to_all(sums_t.astype(jnp.bfloat16), ('cell', 'head'), split_axis=...]
  transfers between devices with their start and end apart: 6 -> 6, of which waited for: 5 -> 5; matrix products, arithmetic and copies ran while one was open for 6% -> 8% of each run, Pallas kernels for 13% -> 13%
where the time goes in v3:
time: 263 us
  waiting for transfers between devices  166 us (63%)
  Pallas kernels  35.2 us (13%)
  starting transfers between devices  15.6 us (6%)
  matrix products  14 us (5%)
  between operations  13.3 us (5%)
  other arithmetic  12.9 us (5%)
  local copies, waits for them, and re-layouts  3.28 us (1%)
    all_to_all x1, waiting for transfers between devices, body(): lax.all_to_all(jnp.broadcast_to(local_queries[None], (n_cell,) + local_qu...  67.1 us
    all_to_all x1, waiting for transfers between devices, body(): lax.all_to_all(sums_t.astype(jnp.bfloat16), ('cell', 'head'), split_axis=...  63 us
    pallas_call x1, Pallas kernels, block_attention(): pl.pallas_call(attention_kernel, grid=(pairs, lat // tile), in_specs=[pl....  35.2 us
    reduce_scatter x1, waiting for transfers between devices, body(): lax.psum_scatter(mlp_part, 'head', scatter_dimension=0, tiled=True)  15.9 us
    all_gather x1, waiting for transfers between devices, body(): lax.all_gather(w_down, 'cell', axis=0, tiled=True)  12.3 us
    all_to_all x1, starting transfers between devices, body(): lax.all_to_all(jnp.broadcast_to(local_queries[None], (n_cell,) + local_qu...  7.41 us
    dot_general x1, matrix products, body(): jnp.dot(hidden, lax.all_gather(w_down, 'cell', axis=0, tiled=True), prefe...  7.1 us
    all_to_all x1, waiting for transfers between devices, body(): lax.all_to_all(ml, ('cell', 'head'), split_axis=1, concat_axis=0, tiled=T...  6.47 us
  transfers between devices with their start and end apart: 6, of which 5 were waited for; matrix products, arithmetic and copies ran while one was open for 8% of the time, Pallas kernels for 13%

profile of v3, /device:TPU:0, one launch (start us, length us, event | category | flops | bytes accessed | tf_op | source)
XLA Modules:
  0.0 262.6 jit_solution(2814982765394567093)
XLA Ops:
  6.5 0.0 copy-start
  6.5 0.0 all-gather.3.cloned.1.call-start
  6.5 0.7 all-gather.3.cloned.1.call-update
  7.3 1.8 convolution_convert_fusion.2
  9.1 1.5 broadcast_in_dim.2
  10.6 0.0 copy-start.3
  10.6 7.4 %all-to-all-start = ((bf16[8,256,512]{2,1,0:T(8,128)(2,1)}), bf16[8,256,512]{2,1,0:T(8,128)(2,1)}, u32[]{:S(2)}, u32[]{:S(2)}) async-start(bf16[8,256,512]{2,1,0:T(8,128)(2,1)} %broadcast_in_dim.2), calls=%async_computation | async-start | bytes 4194304 | tf_op jit(solution)/shard_map/all_to_all | solution.py:66
  18.0 0.0 all-gather.5.cloned.1.call-start
  18.1 0.7 all-gather.5.cloned.1.call-update
  18.8 0.0 copy-done
  18.8 0.0 copy-done.3
  18.8 0.0 copy-start.4
  18.8 2.3 convolution_convert_fusion.vt_ref
  21.1 0.0 copy-done.4
  21.1 2.2 convolution_convert_fusion.1.k_ref
  23.3 67.1 %all-to-all-done = bf16[8,256,512]{2,1,0:T(8,128)(2,1)} async-done(((bf16[8,256,512]{2,1,0:T(8,128)(2,1)}), bf16[8,256,512]{2,1,0:T(8,128)(2,1)}, u32[]{:S(2)}, u32[]{:S(2)}) %all-to-all-start) | async-done | bytes 2097184 | tf_op jit(solution)/shard_map/all_to_all | solution.py:66
  90.4 35.2 %shard_map.82 = (f32[512,2048]{1,0:T(8,128)}, f32[2,4,2,2048]{3,2,1,0:T(2,128)}) custom-call(bf16[2048,512]{1,0:T(8,128)(2,1)} %bitcast.q_ref, bf16[1024,512]{1,0:T(8,128)(2,1)} %convolution_convert_fusion.1.k_ref, bf16[512,1024]{1,0:T(8,128)(2,1)} %convolution_convert_fusion.vt_ref), custom_call_target="tpu_custom_call" | custom-call | tf_op jit(solution)/shard_map/pallas_call | solution.py:40
  125.6 1.0 all_to_all.26
  126.6 0.7 copy.20
  127.3 3.5 %all-to-all-start.1 = ((f32[16,16,128]{2,0,1:T(8,128)}), f32[16,16,128]{2,0,1:T(8,128)S(1)}, u32[]{:S(2)}, u32[]{:S(2)}) async-start(f32[16,16,128]{2,0,1:T(8,128)} %copy.20), calls=%async_computation.1 | async-start | bytes 262144 | tf_op jit(solution)/shard_map/all_to_all | solution.py:84
  130.8 3.9 %copy_bitcast_fusion = bf16[512,16,128]{2,0,1:T(8,128)(2,1)} fusion(f32[512,2048]{1,0:T(8,128)} %get-tuple-element.8), kind=kLoop, calls=%fused_computation.11 | loop fusion | flops 1048576 | bytes 6291456 | tf_op jit(solution)/shard_map/all_to_all | solution.py:81
  134.8 6.5 %all-to-all-done.1 = f32[16,16,128]{2,0,1:T(8,128)S(1)} async-done(((f32[16,16,128]{2,0,1:T(8,128)}), f32[16,16,128]{2,0,1:T(8,128)S(1)}, u32[]{:S(2)}, u32[]{:S(2)}) %all-to-all-start.1) | async-done | bytes 131104 | tf_op jit(solution)/shard_map/all_to_all | solution.py:84
  141.3 4.4 %all-to-all-start.2 = ((bf16[512,16,128]{2,0,1:T(8,128)(2,1)}), bf16[512,16,128]{2,0,1:T(8,128)(2,1)}, u32[]{:S(2)}, u32[]{:S(2)}) async-start(bf16[512,16,128]{2,0,1:T(8,128)(2,1)} %copy_bitcast_fusion), calls=%async_computation.2 | async-start | bytes 4194304 | tf_op jit(solution)/shard_map/all_to_all | solution.py:81
  145.7 0.2 reduce-scatter.2.cloned.1.call-start
  146.0 0.1 fusion.19
  146.1 63.0 %all-to-all-done.2 = bf16[512,16,128]{2,0,1:T(8,128)(2,1)} async-done(((bf16[512,16,128]{2,0,1:T(8,128)(2,1)}), bf16[512,16,128]{2,0,1:T(8,128)(2,1)}, u32[]{:S(2)}, u32[]{:S(2)}) %all-to-all-start.2) | async-done | bytes 2097184 | tf_op jit(solution)/shard_map/all_to_all | solution.py:81
  209.1 2.0 convert_element_type.63
  211.2 0.0 copy-start.1
  211.2 0.0 copy-start.2
  211.2 4.8 %fusion = f32[2,8,64,128]{3,0,2,1:T(2,128)S(1)} fusion(f32[8,2,8,64,128]{4,3,2,1,0:T(8,128)S(1)} %bitcast.38, f32[8,2,8,128]{3,1,0,2:T(2,128)S(1)} %get-tuple-element.10), kind=kLoop, calls=%fused_computation.1 | loop fusion | flops 1966080 | bytes 4784128 | tf_op jit(solution)/shard_map/reduce_sum | solution.py:92
  216.0 0.1 fusion.17
  216.1 0.0 copy-done.1
  216.1 0.0 copy-done.2
  216.1 0.6 multiply_reduce_fusion
  216.7 0.1 multiply_convert_fusion
  216.8 2.2 all_gather.9
  219.0 0.0 all-gather.3.cloned.1.call-done
  219.0 12.3 %all-gather.5.cloned.1.call-done = bf16[2048,1024]{1,0:T(8,128)(2,1)} async-done(((bf16[256,1024]{1,0:T(8,128)(2,1)}), bf16[2048,1024]{1,0:T(8,128)(2,1)}) %all-gather.5.cloned.1.call-update) | async-done | bytes 4194320 | tf_op jit(solution)/shard_map/all_gather | solution.py:119
  231.3 7.1 %fusion.11 = f32[256,1024]{1,0:T(8,128)} fusion(bf16[2048,1024]{1,0:T(8,128)(2,1)} %all-gather.5.cloned.1.call-done, bf16[256,1024]{1,0:T(8,128)(2,1)S(1)} %all_gather.9, bf16[2048,1024]{0,1:T(8,128)(2,1)} %all-gather.3.cloned.1.call-done), kind=kOutput, calls=%fused_computation.19 | convolution fusion | flops 2152202240 | bytes 9961472 | tf_op jit(solution)/shard_map/dot_general | solution.py:117
  238.4 0.0 reduce-scatter.2.cloned.1.call-update
  238.4 15.9 %reduce-scatter.2.cloned.1.call-done = f32[128,1024]{1,0:T(8,128)} async-done(((f32[256,1024]{1,0:T(8,128)}), f32[128,1024]{1,0:T(8,128)}) %reduce-scatter.2.cloned.1.call-update) | async-done | bytes 524304 | tf_op jit(solution)/shard_map/reduce_scatter | solution.py:122
  254.3 1.8 add_convert_fusion
  (4 shorter events, 0.0 us)
Async XLA Ops:
  6.5 12.3 %copy-start = (bf16[1024,1024]{1,0:T(8,128)(2,1)S(1)}, bf16[1024,1024]{1,0:T(8,128)(2,1)}, u32[]{:S(2)}) copy-start(bf16[1024,1024]{1,0:T(8,128)(2,1)} %param.9) | copy-start | bytes 6291460
  6.5 212.4 %all-gather.3.cloned.1.call-start = ((), (), s32[]{:S(2)}) async-start(), calls=%async_computation.4 | async-start | bytes 4718592 | tf_op jit(solution)/shard_map/all_gather | solution.py:111
  10.6 8.2 %copy-start.3 = (bf16[1024,512]{1,0:T(8,128)(2,1)S(1)}, bf16[1024,512]{1,0:T(8,128)(2,1)}, u32[]{:S(2)}) copy-start(bf16[1024,512]{1,0:T(8,128)(2,1)} %param.12) | copy-start | bytes 3145732
  10.6 79.8 %all-to-all-start = ((bf16[8,256,512]{2,1,0:T(8,128)(2,1)}), bf16[8,256,512]{2,1,0:T(8,128)(2,1)}, u32[]{:S(2)}, u32[]{:S(2)}) async-start(bf16[8,256,512]{2,1,0:T(8,128)(2,1)} %broadcast_in_dim.2), calls=%async_computation | async-start | bytes 4194304 | tf_op jit(solution)/shard_map/all_to_all | solution.py:66
  18.0 213.2 %all-gather.5.cloned.1.call-start = ((), (), s32[]{:S(2)}) async-start(), calls=%async_computation.5 | async-start | bytes 4718592 | tf_op jit(solution)/shard_map/all_gather | solution.py:119
  18.8 2.3 copy-start.4
  127.3 13.9 %all-to-all-start.1 = ((f32[16,16,128]{2,0,1:T(8,128)}), f32[16,16,128]{2,0,1:T(8,128)S(1)}, u32[]{:S(2)}, u32[]{:S(2)}) async-start(f32[16,16,128]{2,0,1:T(8,128)} %copy.20), calls=%async_computation.1 | async-start | bytes 262144 | tf_op jit(solution)/shard_map/all_to_all | solution.py:84
  141.3 67.9 %all-to-all-start.2 = ((bf16[512,16,128]{2,0,1:T(8,128)(2,1)}), bf16[512,16,128]{2,0,1:T(8,128)(2,1)}, u32[]{:S(2)}, u32[]{:S(2)}) async-start(bf16[512,16,128]{2,0,1:T(8,128)(2,1)} %copy_bitcast_fusion), calls=%async_computation.2 | async-start | bytes 4194304 | tf_op jit(solution)/shard_map/all_to_all | solution.py:81
  145.7 108.5 %reduce-scatter.2.cloned.1.call-start = ((), (), s32[]{:S(2)}) async-start(), calls=%async_computation.6 | async-start | bytes 1572864 | tf_op jit(solution)/shard_map/reduce_scatter | solution.py:122
  211.2 4.9 %copy-start.1 = (bf16[1024,1024]{1,0:T(8,128)(2,1)S(1)}, bf16[1024,1024]{1,0:T(8,128)(2,1)}, u32[]{:S(2)}) copy-start(bf16[1024,1024]{1,0:T(8,128)(2,1)} %param.13) | copy-start | bytes 6291460
  211.2 4.9 %copy-start.2 = (bf16[256,1024]{1,0:T(8,128)(2,1)S(1)}, bf16[256,1024]{1,0:T(8,128)(2,1)}, u32[]{:S(2)}) copy-start(bf16[256,1024]{1,0:T(8,128)(2,1)} %param.8) | copy-start | bytes 1572868
Sparse Core Ops, SparseCore 0:
  9.4 110.2 all-gather.2
  121.8 109.4 all-gather.4
  238.5 15.7 reduce-scatter.1

commit v4 on v2

--- a/solution.py
+++ b/solution.py
@@ -63,9 +63,9 @@
         jnp.bfloat16
     )
     queries = lax.all_gather(local_queries, "cell", axis=0, tiled=True)
+    n_cell = lax.axis_size("cell")
     lat, width = queries.shape
     heads_local = width // HEAD_DIM
-    n_cell = lax.axis_size("cell")
     n_head = lax.axis_size("head")
     owners = n_cell * n_head
     rows = lat // owners
@@ -98,21 +98,28 @@
     normed = (
         widened * lax.rsqrt(jnp.mean(widened * widened, axis=1, keepdims=True) + 1e-05)
     ).astype(jnp.bfloat16)
+    w_pack = jnp.stack([w_up.T, w_down])
+    w_parts = [w_pack]
+    for k in range(1, n_cell // 2):
+        shift = [(c, (c + 2 * k) % n_cell) for c in range(n_cell)]
+        w_parts.append(lax.ppermute(w_pack, "cell", shift))
+    w_all = jnp.concatenate(w_parts, axis=1)
+    pair = [(c, c ^ 1) for c in range(n_cell)]
     chip_normed = lax.all_gather(normed, "head", axis=0, tiled=True)
+    pair_normed = jnp.concatenate([chip_normed, lax.ppermute(chip_normed, "cell", pair)], axis=0)
     hidden = jax.nn.gelu(
-        jnp.dot(
-            chip_normed,
-            lax.all_gather(w_up, "cell", axis=1, tiled=True),
+        lax.dot_general(
+            pair_normed,
+            w_all[0],
+            (((1,), (1,)), ((), ())),
             preferred_element_type=jnp.float32,
         ),
         approximate=True,
     ).astype(jnp.bfloat16)
-    mlp_part = jnp.dot(
-        hidden,
-        lax.all_gather(w_down, "cell", axis=0, tiled=True),
-        preferred_element_type=jnp.float32,
-    )
-    mlp_out = lax.psum_scatter(mlp_part, "head", scatter_dimension=0, tiled=True)
+    mlp_part = jnp.dot(hidden, w_all[1], preferred_element_type=jnp.float32)
+    chip_rows = chip_normed.shape[0]
+    mlp_chip = mlp_part[:chip_rows] + lax.ppermute(mlp_part[chip_rows:], "cell", pair)
+    mlp_out = lax.psum_scatter(mlp_chip, "head", scatter_dimension=0, tiled=True)
     return (widened + mlp_out).astype(jnp.bfloat16)
 
 

time: 267 us -> 306 us (1.15)
  waiting for transfers between devices: 178 us -> 199 us
  starting transfers between devices: 8.09 us -> 17.6 us
  other arithmetic: 12.8 us -> 18.7 us
    ppermute x0 -> x5, waiting for transfers between devices: none -> 107 us  [the longest x3 84.2 us: body(): w_parts.append(lax.ppermute(w_pack, 'cell', shift))]
    all_gather x2 -> x0, waiting for transfers between devices: 59.5 us -> none  [the longest x1 59.5 us: body(): lax.all_gather(w_down, 'cell', axis=0, tiled=True)]
    all_to_all x1, waiting for transfers between devices: 57.5 us -> 33.8 us  [body(): lax.all_to_all(sums_t.astype(jnp.bfloat16), ('cell', 'head'), split_axis=...]
    ppermute x0 -> x5, starting transfers between devices: none -> 9.59 us  [the longest x3 4.71 us: body(): w_parts.append(lax.ppermute(w_pack, 'cell', shift))]
    concatenate x0 -> x1, other arithmetic: none -> 3.63 us  [body(): w_all = jnp.concatenate(w_parts, axis=1)]
  transfers between devices with their start and end apart: 6 -> 9, of which waited for: 5 -> 7; matrix products, arithmetic and copies ran while one was open for 6% -> 7% of each run, Pallas kernels for 13% -> 0%
where the time goes in v4:
time: 306 us
  waiting for transfers between devices  199 us (65%)
  Pallas kernels  35.2 us (12%)
  other arithmetic  18.7 us (6%)
  starting transfers between devices  17.6 us (6%)
  matrix products  14.1 us (5%)
  between operations  13.6 us (4%)
  local copies, waits for them, and re-layouts  4.48 us (1%)
    ppermute x3, waiting for transfers between devices, body(): w_parts.append(lax.ppermute(w_pack, 'cell', shift))  84.2 us
    all_gather x1, waiting for transfers between devices, body(): queries = lax.all_gather(local_queries, 'cell', axis=0, tiled=True)  47.5 us
    pallas_call x1, Pallas kernels, block_attention(): pl.pallas_call(attention_kernel, grid=(pairs, lat // tile), in_specs=[pl....  35.2 us
    all_to_all x1, waiting for transfers between devices, body(): lax.all_to_all(sums_t.astype(jnp.bfloat16), ('cell', 'head'), split_axis=...  33.8 us
    ppermute x1, waiting for transfers between devices, body(): lax.ppermute(mlp_part[chip_rows:], 'cell', pair)  23.1 us
    reduce_scatter x1, waiting for transfers between devices, body(): lax.psum_scatter(mlp_chip, 'head', scatter_dimension=0, tiled=True)  6.68 us
    dot_general x1, matrix products, body(): mlp_part = jnp.dot(hidden, w_all[1], preferred_element_type=jnp.float32)  6.35 us
  transfers between devices with their start and end apart: 9, of which 7 were waited for; matrix products, arithmetic and copies ran while one was open for 7% of the time, Pallas kernels for 0%

profile of v4, /device:TPU:0, one launch (start us, length us, event | category | flops | bytes accessed | tf_op | source)
XLA Modules:
  0.0 305.6 jit_solution(538520040833207439)
XLA Ops:
  6.5 0.0 copy-start
  6.5 0.0 all-gather.2.cloned.1.call-start
  6.5 2.7 convolution_convert_fusion.2
  9.2 0.0 all-gather.2.cloned.1.call-update
  9.3 0.0 copy-start.8
  9.3 2.2 convolution_convert_fusion.1.k_ref
  11.5 2.3 convolution_convert_fusion.vt_ref
  13.8 47.5 %all-gather.2.cloned.1.call-done.q_ref = bf16[2048,512]{1,0:T(8,128)(2,1)} async-done(((bf16[256,512]{1,0:T(8,128)(2,1)}), bf16[2048,512]{1,0:T(8,128)(2,1)}) %all-gather.2.cloned.1.call-update) | async-done | bytes 2097168 | tf_op jit(solution)/shard_map/all_gather | solution.py:65
  61.3 35.2 %shard_map.82 = (f32[512,2048]{1,0:T(8,128)}, f32[2,4,2,2048]{3,2,1,0:T(2,128)}) custom-call(bf16[2048,512]{1,0:T(8,128)(2,1)} %all-gather.2.cloned.1.call-done.q_ref, bf16[1024,512]{1,0:T(8,128)(2,1)} %convolution_convert_fusion.1.k_ref, bf16[512,1024]{1,0:T(8,128)(2,1)} %convolution_convert_fusion.vt_ref), custom_call_target="tpu_custom_call" | custom-call | tf_op jit(solution)/shard_map/pallas_call | solution.py:40
  96.6 1.0 all_to_all.22
  97.6 0.7 copy.23
  98.3 3.5 %all-to-all-start = ((f32[16,16,128]{2,0,1:T(8,128)}), f32[16,16,128]{2,0,1:T(8,128)S(1)}, u32[]{:S(2)}, u32[]{:S(2)}) async-start(f32[16,16,128]{2,0,1:T(8,128)} %copy.23), calls=%async_computation | async-start | bytes 262144 | tf_op jit(solution)/shard_map/all_to_all | solution.py:78
  101.8 3.9 %copy_bitcast_fusion = bf16[512,16,128]{2,0,1:T(8,128)(2,1)} fusion(f32[512,2048]{1,0:T(8,128)} %get-tuple-element.8), kind=kLoop, calls=%fused_computation.12 | loop fusion | flops 1048576 | bytes 6291456 | tf_op jit(solution)/shard_map/all_to_all | solution.py:75
  105.7 3.9 %all-to-all-done = f32[16,16,128]{2,0,1:T(8,128)S(1)} async-done(((f32[16,16,128]{2,0,1:T(8,128)}), f32[16,16,128]{2,0,1:T(8,128)S(1)}, u32[]{:S(2)}, u32[]{:S(2)}) %all-to-all-start) | async-done | bytes 131104 | tf_op jit(solution)/shard_map/all_to_all | solution.py:78
  109.7 4.4 %all-to-all-start.1 = ((bf16[512,16,128]{2,0,1:T(8,128)(2,1)}), bf16[512,16,128]{2,0,1:T(8,128)(2,1)}, u32[]{:S(2)}, u32[]{:S(2)}) async-start(bf16[512,16,128]{2,0,1:T(8,128)(2,1)} %copy_bitcast_fusion), calls=%async_computation.1 | async-start | bytes 4194304 | tf_op jit(solution)/shard_map/all_to_all | solution.py:75
  114.1 0.0 reduce-scatter.2.cloned.1.call-start
  114.1 1.2 copy.30
  115.4 1.1 pad_maximum_fusion.1
  116.5 3.6 %collective-permute-start.3 = (bf16[2,256,1024]{2,1,0:T(8,128)(2,1)}, bf16[2,256,1024]{2,1,0:T(8,128)(2,1)}, u32[]{:S(2)}, u32[]{:S(2)}) collective-permute-start(bf16[2,256,1024]{2,1,0:T(8,128)(2,1)} %pad_maximum_fusion.1), channel_id=1, source_target_pairs={{0,12},{2,14},{4,0},{6,2},{8,4},{10,6},{12,8},{14,10},{1,13},{3,15... | collective-permute-start | bytes 3145736 | tf_op jit(solution)/shard_map/ppermute | solution.py:105
  120.1 0.0 collective-permute-start.2
  120.1 1.1 collective-permute-start.1
  121.2 0.1 fusion.25
  121.3 33.8 %all-to-all-done.1 = bf16[512,16,128]{2,0,1:T(8,128)(2,1)} async-done(((bf16[512,16,128]{2,0,1:T(8,128)(2,1)}), bf16[512,16,128]{2,0,1:T(8,128)(2,1)}, u32[]{:S(2)}, u32[]{:S(2)}) %all-to-all-start.1) | async-done | bytes 2097184 | tf_op jit(solution)/shard_map/all_to_all | solution.py:75
  155.1 2.0 convert_element_type.63
  157.1 0.0 copy-start.2
  157.1 0.0 copy-start.5
  157.1 4.8 %fusion = f32[2,8,64,128]{3,0,2,1:T(2,128)S(1)} fusion(f32[8,2,8,64,128]{4,3,2,1,0:T(8,128)S(1)} %bitcast.47, f32[8,2,8,128]{3,1,0,2:T(2,128)S(1)} %get-tuple-element.10), kind=kLoop, calls=%fused_computation.2 | loop fusion | flops 1966080 | bytes 4784128 | tf_op jit(solution)/shard_map/reduce_sum | solution.py:86
  162.0 0.1 fusion.23
  162.0 0.0 copy-done.2
  162.0 0.0 copy-done.5
  162.0 0.0 copy-start.4
  162.1 0.6 multiply_reduce_fusion
  162.6 0.1 multiply_convert_fusion
  162.7 2.8 all_gather.7
  165.5 3.3 %collective-permute-start = (bf16[256,1024]{1,0:T(8,128)(2,1)S(1)}, bf16[256,1024]{1,0:T(8,128)(2,1)}, u32[]{:S(2)}, u32[]{:S(2)}) collective-permute-start(bf16[256,1024]{1,0:T(8,128)(2,1)S(1)} %all_gather.7), channel_id=1, source_target_pairs={{0,2},{2,0},{4,6},{6,4},{8,10},{10,8},{12,14},{14,12},{1,3},{3,1},... | collective-permute-start | bytes 1572872 | tf_op jit(solution)/shard_map/ppermute | solution.py:109
  168.8 4.5 %collective-permute-done.3 = bf16[2,256,1024]{2,1,0:T(8,128)(2,1)} collective-permute-done((bf16[2,256,1024]{2,1,0:T(8,128)(2,1)}, bf16[2,256,1024]{2,1,0:T(8,128)(2,1)}, u32[]{:S(2)}, u32[]{:S(2)}) %collective-permute-start.3) | collective-permute-done | bytes 1048608 | tf_op jit(solution)/shard_map/ppermute | solution.py:105
  173.3 79.7 %collective-permute-done.2 = bf16[2,256,1024]{2,1,0:T(8,128)(2,1)} collective-permute-done((bf16[2,256,1024]{2,1,0:T(8,128)(2,1)}, bf16[2,256,1024]{2,1,0:T(8,128)(2,1)}, u32[]{:S(2)}, u32[]{:S(2)}) %collective-permute-start.2) | collective-permute-done | bytes 1048608 | tf_op jit(solution)/shard_map/ppermute | solution.py:105
  253.0 0.0 collective-permute-done.1
  253.0 3.6 %pad_maximum_fusion = bf16[2,1024,1024]{2,1,0:T(8,128)(2,1)} fusion(bf16[2,256,1024]{2,1,0:T(8,128)(2,1)} %collective-permute-done.3, bf16[2,256,1024]{2,1,0:T(8,128)(2,1)} %collective-permute-done.2, bf16[2,256,1024]{2,1,0:T(8,128)(2,1)} %collective-permute-done.1, bf16[1,256,1024]{2,1,0:T(8,128)(2,1)S(1)} %bitcast.51, bf16[1,256,1024]{2,1,0:T(8,128)(2,1)S(1)} %bitcast.49), kind=kLoop, calls=%fused_computation | loop fusion | flops 20971520 | bytes 8388608 | tf_op jit(solution)/shard_map/concatenate | solution.py:106
  256.7 0.0 collective-permute-done
  256.7 6.3 %fusion.9 = f32[512,1024]{1,0:T(8,128)} fusion(bf16[2,1024,1024]{2,1,0:T(8,128)(2,1)} %pad_maximum_fusion, bf16[256,1024]{1,0:T(8,128)(2,1)} %collective-permute-done, bf16[256,1024]{1,0:T(8,128)(2,1)} %copy-done.6), kind=kOutput, calls=%fused_computation.14 | convolution fusion | flops 2154299392 | bytes 7340032 | tf_op jit(solution)/shard_map/dot_general | solution.py:119
  263.0 1.5 slice.29
  264.5 1.5 collective-permute-start.4
  266.0 23.1 %collective-permute-done.4 = f32[256,1024]{1,0:T(8,128)S(1)} collective-permute-done((f32[256,1024]{1,0:T(8,128)S(1)}, f32[256,1024]{1,0:T(8,128)S(1)}, u32[]{:S(2)}, u32[]{:S(2)}) %collective-permute-start.4) | collective-permute-done | bytes 1048608 | tf_op jit(solution)/shard_map/ppermute | solution.py:121
  289.2 1.1 slice_add_fusion
  290.3 0.0 reduce-scatter.2.cloned.1.call-update
  290.3 6.7 %reduce-scatter.2.cloned.1.call-done = f32[128,1024]{1,0:T(8,128)} async-done(((f32[256,1024]{1,0:T(8,128)}), f32[128,1024]{1,0:T(8,128)}) %reduce-scatter.2.cloned.1.call-update) | async-done | bytes 524304 | tf_op jit(solution)/shard_map/reduce_scatter | solution.py:122
  297.0 1.8 add_convert_fusion
  (15 shorter events, 0.1 us)
Async XLA Ops:
  6.5 2.7 copy-start
  6.5 2.7 copy-start.7
  6.5 54.8 %all-gather.2.cloned.1.call-start = ((), (), s32[]{:S(2)}) async-start(), calls=%async_computation.3 | async-start | bytes 2359296 | tf_op jit(solution)/shard_map/all_gather | solution.py:65
  9.3 2.3 copy-start.8
  98.3 11.4 %all-to-all-start = ((f32[16,16,128]{2,0,1:T(8,128)}), f32[16,16,128]{2,0,1:T(8,128)S(1)}, u32[]{:S(2)}, u32[]{:S(2)}) async-start(f32[16,16,128]{2,0,1:T(8,128)} %copy.23), calls=%async_computation | async-start | bytes 262144 | tf_op jit(solution)/shard_map/all_to_all | solution.py:78
  105.7 9.7 %copy-start.3 = (bf16[256,1024]{1,0:T(8,128)(2,1)S(1)}, bf16[256,1024]{1,0:T(8,128)(2,1)}, u32[]{:S(2)}) copy-start(bf16[256,1024]{1,0:T(8,128)(2,1)} %param.15) | copy-start | bytes 1572868
  109.7 45.4 %all-to-all-start.1 = ((bf16[512,16,128]{2,0,1:T(8,128)(2,1)}), bf16[512,16,128]{2,0,1:T(8,128)(2,1)}, u32[]{:S(2)}, u32[]{:S(2)}) async-start(bf16[512,16,128]{2,0,1:T(8,128)(2,1)} %copy_bitcast_fusion), calls=%async_computation.1 | async-start | bytes 4194304 | tf_op jit(solution)/shard_map/all_to_all | solution.py:75
  114.1 182.9 %reduce-scatter.2.cloned.1.call-start = ((), (), s32[]{:S(2)}) async-start(), calls=%async_computation.4 | async-start | bytes 1572864 | tf_op jit(solution)/shard_map/reduce_scatter | solution.py:122
  116.5 56.8 %collective-permute-start.3 = (bf16[2,256,1024]{2,1,0:T(8,128)(2,1)}, bf16[2,256,1024]{2,1,0:T(8,128)(2,1)}, u32[]{:S(2)}, u32[]{:S(2)}) collective-permute-start(bf16[2,256,1024]{2,1,0:T(8,128)(2,1)} %pad_maximum_fusion.1), channel_id=1, source_target_pairs={{0,12},{2,14},{4,0},{6,2},{8,4},{10,6},{12,8},{14,10},{1,13},{3,15... | collective-permute-start | bytes 3145736 | tf_op jit(solution)/shard_map/ppermute | solution.py:105
  120.1 132.9 %collective-permute-start.2 = (bf16[2,256,1024]{2,1,0:T(8,128)(2,1)}, bf16[2,256,1024]{2,1,0:T(8,128)(2,1)}, u32[]{:S(2)}, u32[]{:S(2)}) collective-permute-start(bf16[2,256,1024]{2,1,0:T(8,128)(2,1)} %pad_maximum_fusion.1), channel_id=1, source_target_pairs={{0,8},{2,10},{4,12},{6,14},{8,0},{10,2},{12,4},{14,6},{1,9},{3,11}... | collective-permute-start | bytes 3145736 | tf_op jit(solution)/shard_map/ppermute | solution.py:105
  120.1 132.9 %collective-permute-start.1 = (bf16[2,256,1024]{2,1,0:T(8,128)(2,1)}, bf16[2,256,1024]{2,1,0:T(8,128)(2,1)}, u32[]{:S(2)}, u32[]{:S(2)}) collective-permute-start(bf16[2,256,1024]{2,1,0:T(8,128)(2,1)} %pad_maximum_fusion.1), channel_id=1, source_target_pairs={{0,4},{2,6},{4,8},{6,10},{8,12},{10,14},{12,0},{14,2},{1,5},{3,7},... | collective-permute-start | bytes 3145736 | tf_op jit(solution)/shard_map/ppermute | solution.py:105
  157.1 4.9 %copy-start.2 = (bf16[1024,1024]{1,0:T(8,128)(2,1)S(1)}, bf16[1024,1024]{1,0:T(8,128)(2,1)}, u32[]{:S(2)}) copy-start(bf16[1024,1024]{1,0:T(8,128)(2,1)} %param.13) | copy-start | bytes 6291460
  157.1 4.9 %copy-start.5 = (bf16[256,1024]{1,0:T(8,128)(2,1)S(1)}, bf16[256,1024]{1,0:T(8,128)(2,1)}, u32[]{:S(2)}) copy-start(bf16[256,1024]{1,0:T(8,128)(2,1)} %param.8) | copy-start | bytes 1572868
  162.0 91.0 %copy-start.4 = (bf16[256,1024]{1,0:T(8,128)(2,1)S(1)}, bf16[256,1024]{1,0:T(8,128)(2,1)}, u32[]{:S(2)}) copy-start(bf16[256,1024]{1,0:T(8,128)(2,1)} %param.15) | copy-start | bytes 1572868
  165.5 91.2 %copy-start.6 = (bf16[256,1024]{1,0:T(8,128)(2,1)}, bf16[256,1024]{1,0:T(8,128)(2,1)S(1)}, u32[]{:S(2)}) copy-start(bf16[256,1024]{1,0:T(8,128)(2,1)S(1)} %all_gather.7) | copy-start | bytes 1572868
  165.5 91.2 %collective-permute-start = (bf16[256,1024]{1,0:T(8,128)(2,1)S(1)}, bf16[256,1024]{1,0:T(8,128)(2,1)}, u32[]{:S(2)}, u32[]{:S(2)}) collective-permute-start(bf16[256,1024]{1,0:T(8,128)(2,1)S(1)} %all_gather.7), channel_id=1, source_target_pairs={{0,2},{2,0},{4,6},{6,4},{8,10},{10,8},{12,14},{14,12},{1,3},{3,1},... | collective-permute-start | bytes 1572872 | tf_op jit(solution)/shard_map/ppermute | solution.py:109
  263.0 26.2 %copy-start.1 = (f32[512,1024]{1,0:T(8,128)S(1)}, f32[512,1024]{1,0:T(8,128)}, u32[]{:S(2)}) copy-start(f32[512,1024]{1,0:T(8,128)} %fusion.9) | copy-start | bytes 6291460
  264.5 24.7 %collective-permute-start.4 = (f32[256,1024]{1,0:T(8,128)S(1)}, f32[256,1024]{1,0:T(8,128)S(1)}, u32[]{:S(2)}, u32[]{:S(2)}) collective-permute-start(f32[256,1024]{1,0:T(8,128)S(1)} %slice.29), channel_id=1, source_target_pairs={{0,2},{2,0},{4,6},{6,4},{8,10},{10,8},{12,14},{14,12},{1,3},{3,1},... | collective-permute-start | bytes 3145736 | tf_op jit(solution)/shard_map/ppermute | solution.py:121
Sparse Core Ops, SparseCore 0:
  9.5 51.7 all-gather.1
  290.4 6.5 reduce-scatter.1

commit v5 on v2

--- a/solution.py
+++ b/solution.py
@@ -5,9 +5,11 @@
 from jax import lax
 from jax.experimental import pallas as pl
 from jax.experimental.pallas import tpu as pltpu
+from jax.sharding import Mesh
 from jax.sharding import PartitionSpec as P
 
 HEAD_DIM = 64
+CELL = ("cz", "cx")
 LAT_TILE = 512
 
 
@@ -62,10 +64,10 @@
     local_queries = jnp.dot(latents, w_query, preferred_element_type=jnp.float32).astype(
         jnp.bfloat16
     )
-    queries = lax.all_gather(local_queries, "cell", axis=0, tiled=True)
+    queries = lax.all_gather(local_queries, CELL, axis=0, tiled=True)
+    n_cell = lax.axis_size(CELL)
     lat, width = queries.shape
     heads_local = width // HEAD_DIM
-    n_cell = lax.axis_size("cell")
     n_head = lax.axis_size("head")
     owners = n_cell * n_head
     rows = lat // owners
@@ -73,9 +75,9 @@
     sums_t, ml = block_attention(queries, key_rows, value_t)
     ml = ml.reshape(2 * heads_local, lat)
     sums_recv = lax.all_to_all(
-        sums_t.astype(jnp.bfloat16), ("cell", "head"), split_axis=1, concat_axis=0, tiled=True
+        sums_t.astype(jnp.bfloat16), CELL + ("head",), split_axis=1, concat_axis=0, tiled=True
     )
-    ml_recv = lax.all_to_all(ml, ("cell", "head"), split_axis=1, concat_axis=0, tiled=True)
+    ml_recv = lax.all_to_all(ml, CELL + ("head",), split_axis=1, concat_axis=0, tiled=True)
     sums_recv = sums_recv.reshape(n_cell, n_head, heads_local, HEAD_DIM, rows).astype(jnp.float32)
     ml_recv = ml_recv.reshape(n_cell, n_head, 2, heads_local, rows)
     block_max = ml_recv[:, :, 0]
@@ -87,7 +89,7 @@
     attended_t = summed / totals[:, :, None, :]
     attended = attended_t.reshape(n_head * width, rows).T.astype(jnp.bfloat16)
 
-    own_index = lax.axis_index("cell") * n_head + lax.axis_index("head")
+    own_index = lax.axis_index(CELL) * n_head + lax.axis_index("head")
     local_rows = latents.shape[0]
     own_latents = lax.dynamic_slice_in_dim(
         latents, (own_index % (local_rows // rows)) * rows, rows, 0
@@ -98,38 +100,40 @@
     normed = (
         widened * lax.rsqrt(jnp.mean(widened * widened, axis=1, keepdims=True) + 1e-05)
     ).astype(jnp.bfloat16)
+    w_pack = lax.all_gather(jnp.stack([w_up.T, w_down]), "cz", axis=1, tiled=True)
     chip_normed = lax.all_gather(normed, "head", axis=0, tiled=True)
+    pair_normed = lax.all_gather(chip_normed, "cx", axis=0, tiled=True)
     hidden = jax.nn.gelu(
-        jnp.dot(
-            chip_normed,
-            lax.all_gather(w_up, "cell", axis=1, tiled=True),
+        lax.dot_general(
+            pair_normed,
+            w_pack[0],
+            (((1,), (1,)), ((), ())),
             preferred_element_type=jnp.float32,
         ),
         approximate=True,
     ).astype(jnp.bfloat16)
-    mlp_part = jnp.dot(
-        hidden,
-        lax.all_gather(w_down, "cell", axis=0, tiled=True),
-        preferred_element_type=jnp.float32,
-    )
-    mlp_out = lax.psum_scatter(mlp_part, "head", scatter_dimension=0, tiled=True)
+    mlp_part = jnp.dot(hidden, w_pack[1], preferred_element_type=jnp.float32)
+    mlp_out = lax.psum_scatter(mlp_part, ("cx", "head"), scatter_dimension=0, tiled=True)
     return (widened + mlp_out).astype(jnp.bfloat16)
 
 
 def solution(mesh):
+    assert tuple(mesh.axis_names) == ("group", "cell", "head")
+    sizes = (mesh.shape["group"], mesh.shape["cell"] // 2, 2, mesh.shape["head"])
+    split = Mesh(mesh.devices.reshape(sizes), ("group",) + CELL + ("head",))
     return jax.shard_map(
         body,
-        mesh=mesh,
+        mesh=split,
         in_specs=(
-            P(("group", "cell"), None),
-            P(("group", "cell"), None),
+            P(("group",) + CELL, None),
+            P(("group",) + CELL, None),
             P(None, "head"),
             P(None, "head"),
             P(None, "head"),
             P(),
-            P(None, ("cell", "head")),
-            P(("cell", "head"), None),
+            P(None, CELL + ("head",)),
+            P(CELL + ("head",), None),
         ),
-        out_specs=P(("group", "cell", "head"), None),
+        out_specs=P(("group",) + CELL + ("head",), None),
         check_vma=False,
     )

time: 267 us -> 266 us (level)
  waiting for transfers between devices: 178 us -> 174 us
    all_gather x3, waiting for transfers between devices: 105 us -> 71 us  [the longest x1 43.7 us: body(): queries = lax.all_gather(local_queries, CELL, axis=0, tiled=True)]
    reduce_scatter x1, waiting for transfers between devices: 7.07 us -> 31.3 us  [body(): lax.psum_scatter(mlp_part, ('cx', 'head'), scatter_dimension=0, tiled=True)]
    all_to_all x2, waiting for transfers between devices: 63.9 us -> 71.5 us  [the longest x1 65 us: body(): lax.all_to_all(sums_t.astype(jnp.bfloat16), CELL + ('head',), split_axis=...]
  transfers between devices with their start and end apart: 6 -> 6, of which waited for: 5 -> 5; matrix products, arithmetic and copies ran while one was open for 6% -> 8% of each run, Pallas kernels for 13% -> 13%
where the time goes in v5:
time: 266 us; the launch traced here: 265 us
  waiting for transfers between devices  174 us (65%)
  Pallas kernels  35.2 us (13%)
  matrix products  15.5 us (6%)
  other arithmetic  15 us (6%)
  between operations  13.3 us (5%)
  starting transfers between devices  8.07 us (3%)
    all_to_all x1, waiting for transfers between devices, body(): lax.all_to_all(sums_t.astype(jnp.bfloat16), CELL + ('head',), split_axis=...  65 us
    all_gather x1, waiting for transfers between devices, body(): queries = lax.all_gather(local_queries, CELL, axis=0, tiled=True)  43.7 us
    pallas_call x1, Pallas kernels, block_attention(): pl.pallas_call(attention_kernel, grid=(pairs, lat // tile), in_specs=[pl....  35.2 us
    reduce_scatter x1, waiting for transfers between devices, body(): lax.psum_scatter(mlp_part, ('cx', 'head'), scatter_dimension=0, tiled=True)  31.3 us
    all_gather x1, waiting for transfers between devices, body(): pair_normed = lax.all_gather(chip_normed, 'cx', axis=0, tiled=True)  27.3 us
    all_to_all x1, waiting for transfers between devices, body(): lax.all_to_all(ml, CELL + ('head',), split_axis=1, concat_axis=0, tiled=T...  6.43 us
    dot_general x1, matrix products, body(): mlp_part = jnp.dot(hidden, w_pack[1], preferred_element_type=jnp.float32)  6.33 us
  transfers between devices with their start and end apart: 6, of which 5 were waited for; matrix products, arithmetic and copies ran while one was open for 8% of the time, Pallas kernels for 13%

profile of v5, /device:TPU:0, one launch (start us, length us, event | category | flops | bytes accessed | tf_op | source)
XLA Modules:
  0.0 265.2 jit_solution(6821583866735699027)
XLA Ops:
  6.5 0.0 copy-start
  6.5 0.0 copy-start.3
  6.5 0.0 all-gather.4.cloned.1.call-start
  6.5 2.7 %convolution_convert_fusion.2 = bf16[256,512]{1,0:T(8,128)(2,1)} fusion(bf16[256,1024]{1,0:T(8,128)(2,1)} %param.8, bf16[1024,512]{1,0:T(8,128)(2,1)} %param.10), kind=kOutput, calls=%fused_computation.20 | convolution fusion | flops 268566528 | bytes 1835008 | tf_op jit(solution)/shard_map/dot_general | solution.py:64
  9.2 0.0 all-gather.4.cloned.1.call-update
  9.2 0.0 all-gather.8.cloned.1.call-start
  9.3 0.0 copy-done.3
  9.3 0.2 copy.30
  9.5 2.1 pad_maximum_fusion
  11.6 0.0 all-gather.8.cloned.1.call-update
  11.7 0.0 copy-done
  11.7 0.0 copy-start.4
  11.7 3.6 %convolution_convert_fusion.1.k_ref = bf16[1024,512]{1,0:T(8,128)(2,1)} fusion(bf16[1024,1024]{1,0:T(8,128)(2,1)S(1)} %copy-done, bf16[1024,512]{1,0:T(8,128)(2,1)} %param.11), kind=kOutput, calls=%fused_computation.18 | convolution fusion | flops 1074266112 | bytes 4194304 | tf_op jit(solution)/shard_map/dot_general | solution.py:62
  15.3 0.0 copy-done.4
  15.3 2.4 convolution_convert_fusion.vt_ref
  17.6 43.7 %all-gather.4.cloned.1.call-done.q_ref = bf16[2048,512]{1,0:T(8,128)(2,1)} async-done(((bf16[256,512]{1,0:T(8,128)(2,1)}), bf16[2048,512]{1,0:T(8,128)(2,1)}) %all-gather.4.cloned.1.call-update) | async-done | bytes 2097168 | tf_op jit(solution)/shard_map/all_gather | solution.py:67
  61.3 35.2 %shard_map.82 = (f32[512,2048]{1,0:T(8,128)}, f32[2,4,2,2048]{3,2,1,0:T(2,128)}) custom-call(bf16[2048,512]{1,0:T(8,128)(2,1)} %all-gather.4.cloned.1.call-done.q_ref, bf16[1024,512]{1,0:T(8,128)(2,1)} %convolution_convert_fusion.1.k_ref, bf16[512,1024]{1,0:T(8,128)(2,1)} %convolution_convert_fusion.vt_ref), custom_call_target="tpu_custom_call" | custom-call | tf_op jit(solution)/shard_map/pallas_call | solution.py:42
  96.5 1.0 all_to_all.22
  97.5 0.7 copy.23
  98.2 3.5 %all-to-all-start = ((f32[16,16,128]{2,0,1:T(8,128)}), f32[16,16,128]{2,0,1:T(8,128)S(1)}, u32[]{:S(2)}, u32[]{:S(2)}) async-start(f32[16,16,128]{2,0,1:T(8,128)} %copy.23), calls=%async_computation | async-start | bytes 262144 | tf_op jit(solution)/shard_map/all_to_all | solution.py:80
  101.8 4.0 %copy_bitcast_fusion = bf16[512,16,128]{2,0,1:T(8,128)(2,1)} fusion(f32[512,2048]{1,0:T(8,128)} %get-tuple-element.8), kind=kLoop, calls=%fused_computation.11 | loop fusion | flops 1048576 | bytes 6291456 | tf_op jit(solution)/shard_map/all_to_all | solution.py:77
  105.7 6.4 %all-to-all-done = f32[16,16,128]{2,0,1:T(8,128)S(1)} async-done(((f32[16,16,128]{2,0,1:T(8,128)}), f32[16,16,128]{2,0,1:T(8,128)S(1)}, u32[]{:S(2)}, u32[]{:S(2)}) %all-to-all-start) | async-done | bytes 131104 | tf_op jit(solution)/shard_map/all_to_all | solution.py:80
  112.2 4.4 %all-to-all-start.1 = ((bf16[512,16,128]{2,0,1:T(8,128)(2,1)}), bf16[512,16,128]{2,0,1:T(8,128)(2,1)}, u32[]{:S(2)}, u32[]{:S(2)}) async-start(bf16[512,16,128]{2,0,1:T(8,128)(2,1)} %copy_bitcast_fusion), calls=%async_computation.1 | async-start | bytes 4194304 | tf_op jit(solution)/shard_map/all_to_all | solution.py:77
  116.6 0.0 all-gather.6.cloned.1.call-start
  116.7 0.1 fusion.19
  116.8 65.0 %all-to-all-done.1 = bf16[512,16,128]{2,0,1:T(8,128)(2,1)} async-done(((bf16[512,16,128]{2,0,1:T(8,128)(2,1)}), bf16[512,16,128]{2,0,1:T(8,128)(2,1)}, u32[]{:S(2)}, u32[]{:S(2)}) %all-to-all-start.1) | async-done | bytes 2097184 | tf_op jit(solution)/shard_map/all_to_all | solution.py:77
  181.8 2.0 convert_element_type.63
  183.9 0.0 copy-start.1
  183.9 0.0 copy-start.2
  183.9 4.8 %fusion = f32[2,8,64,128]{3,0,2,1:T(2,128)S(1)} fusion(f32[8,2,8,64,128]{4,3,2,1,0:T(8,128)S(1)} %bitcast.48, f32[8,2,8,128]{3,1,0,2:T(2,128)S(1)} %get-tuple-element.10), kind=kLoop, calls=%fused_computation.1 | loop fusion | flops 1966080 | bytes 4784128 | tf_op jit(solution)/shard_map/reduce_sum | solution.py:88
  188.7 0.1 fusion.17
  188.8 0.0 copy-done.1
  188.8 0.0 copy-done.2
  188.8 0.6 multiply_reduce_fusion
  189.4 0.1 multiply_convert_fusion
  189.5 2.3 all_gather.13
  191.8 0.0 all-gather.6.cloned.1.call-update
  191.8 0.0 reduce-scatter.2.cloned.1.call-start
  191.9 0.0 all-gather.8.cloned.1.call-done
  191.9 27.3 %all-gather.6.cloned.1.call-done = bf16[512,1024]{1,0:T(8,128)(2,1)} async-done(((bf16[256,1024]{1,0:T(8,128)(2,1)}), bf16[512,1024]{1,0:T(8,128)(2,1)}) %all-gather.6.cloned.1.call-update) | async-done | bytes 1048592 | tf_op jit(solution)/shard_map/all_gather | solution.py:105
  219.2 6.3 %fusion.9 = f32[512,1024]{1,0:T(8,128)} fusion(bf16[2,1024,1024]{2,1,0:T(8,128)(2,1)} %all-gather.8.cloned.1.call-done, bf16[512,1024]{1,0:T(8,128)(2,1)} %all-gather.6.cloned.1.call-done), kind=kOutput, calls=%fused_computation.13 | convolution fusion | flops 2152202240 | bytes 7340032 | tf_op jit(solution)/shard_map/dot_general | solution.py:115
  225.5 0.0 reduce-scatter.2.cloned.1.call-update
  225.6 31.3 %reduce-scatter.2.cloned.1.call-done = f32[128,1024]{1,0:T(8,128)} async-done(((f32[512,1024]{1,0:T(8,128)}), f32[128,1024]{1,0:T(8,128)}) %reduce-scatter.2.cloned.1.call-update) | async-done | bytes 524304 | tf_op jit(solution)/shard_map/reduce_scatter | solution.py:116
  256.9 1.8 add_convert_fusion
  (4 shorter events, 0.0 us)
Async XLA Ops:
  6.5 5.1 %copy-start = (bf16[1024,1024]{1,0:T(8,128)(2,1)S(1)}, bf16[1024,1024]{1,0:T(8,128)(2,1)}, u32[]{:S(2)}) copy-start(bf16[1024,1024]{1,0:T(8,128)(2,1)} %param.9) | copy-start | bytes 6291460
  6.5 2.8 %copy-start.3 = (bf16[1024,256]{1,0:T(8,128)(2,1)S(1)}, bf16[1024,256]{1,0:T(8,128)(2,1)}, u32[]{:S(2)}) copy-start(bf16[1024,256]{1,0:T(8,128)(2,1)} %param.14) | copy-start | bytes 1572868
  6.5 54.8 %all-gather.4.cloned.1.call-start = ((), (), s32[]{:S(2)}) async-start(), calls=%async_computation.3 | async-start | bytes 2359296 | tf_op jit(solution)/shard_map/all_gather | solution.py:67
  9.2 182.6 %all-gather.8.cloned.1.call-start = ((), (), s32[]{:S(2)}) async-start(), calls=%async_computation.5 | async-start | bytes 5242880 | tf_op jit(solution)/shard_map/all_gather | solution.py:103
  11.7 3.6 %copy-start.4 = (bf16[1024,512]{1,0:T(8,128)(2,1)S(1)}, bf16[1024,512]{1,0:T(8,128)(2,1)}, u32[]{:S(2)}) copy-start(bf16[1024,512]{1,0:T(8,128)(2,1)} %param.12) | copy-start | bytes 3145732
  98.2 13.9 %all-to-all-start = ((f32[16,16,128]{2,0,1:T(8,128)}), f32[16,16,128]{2,0,1:T(8,128)S(1)}, u32[]{:S(2)}, u32[]{:S(2)}) async-start(f32[16,16,128]{2,0,1:T(8,128)} %copy.23), calls=%async_computation | async-start | bytes 262144 | tf_op jit(solution)/shard_map/all_to_all | solution.py:80
  112.2 69.7 %all-to-all-start.1 = ((bf16[512,16,128]{2,0,1:T(8,128)(2,1)}), bf16[512,16,128]{2,0,1:T(8,128)(2,1)}, u32[]{:S(2)}, u32[]{:S(2)}) async-start(bf16[512,16,128]{2,0,1:T(8,128)(2,1)} %copy_bitcast_fusion), calls=%async_computation.1 | async-start | bytes 4194304 | tf_op jit(solution)/shard_map/all_to_all | solution.py:77
  116.6 102.6 %all-gather.6.cloned.1.call-start = ((), (), s32[]{:S(2)}) async-start(), calls=%async_computation.4 | async-start | bytes 1572864 | tf_op jit(solution)/shard_map/all_gather | solution.py:105
  183.9 4.9 %copy-start.1 = (bf16[1024,1024]{1,0:T(8,128)(2,1)S(1)}, bf16[1024,1024]{1,0:T(8,128)(2,1)}, u32[]{:S(2)}) copy-start(bf16[1024,1024]{1,0:T(8,128)(2,1)} %param.13) | copy-start | bytes 6291460
  183.9 4.9 %copy-start.2 = (bf16[256,1024]{1,0:T(8,128)(2,1)S(1)}, bf16[256,1024]{1,0:T(8,128)(2,1)}, u32[]{:S(2)}) copy-start(bf16[256,1024]{1,0:T(8,128)(2,1)} %param.8) | copy-start | bytes 1572868
  191.8 65.1 %reduce-scatter.2.cloned.1.call-start = ((), (), s32[]{:S(2)}) async-start(), calls=%async_computation.6 | async-start | bytes 2621440 | tf_op jit(solution)/shard_map/reduce_scatter | solution.py:116
Sparse Core Ops, SparseCore 0:
  9.5 51.7 all-gather.3
  62.9 117.1 all-gather.7
  191.9 27.2 all-gather.5
  225.7 31.1 reduce-scatter.1

commit v6 on v5

--- a/solution.py
+++ b/solution.py
@@ -102,7 +102,8 @@
     ).astype(jnp.bfloat16)
     w_pack = lax.all_gather(jnp.stack([w_up.T, w_down]), "cz", axis=1, tiled=True)
     chip_normed = lax.all_gather(normed, "head", axis=0, tiled=True)
-    pair_normed = lax.all_gather(chip_normed, "cx", axis=0, tiled=True)
+    swap = [(0, 1), (1, 0)]
+    pair_normed = jnp.concatenate([chip_normed, lax.ppermute(chip_normed, "cx", swap)], axis=0)
     hidden = jax.nn.gelu(
         lax.dot_general(
             pair_normed,
@@ -113,7 +114,9 @@
         approximate=True,
     ).astype(jnp.bfloat16)
     mlp_part = jnp.dot(hidden, w_pack[1], preferred_element_type=jnp.float32)
-    mlp_out = lax.psum_scatter(mlp_part, ("cx", "head"), scatter_dimension=0, tiled=True)
+    chip_rows = chip_normed.shape[0]
+    mlp_chip = mlp_part[:chip_rows] + lax.ppermute(mlp_part[chip_rows:], "cx", swap)
+    mlp_out = lax.psum_scatter(mlp_chip, "head", scatter_dimension=0, tiled=True)
     return (widened + mlp_out).astype(jnp.bfloat16)
 
 

time: 266 us -> 262 us (0.985)
  waiting for transfers between devices: 174 us -> 163 us
  starting transfers between devices: 8.07 us -> 13.2 us
    ppermute x0 -> x2, waiting for transfers between devices: none -> 35.2 us  [the longest x1 22.9 us: body(): lax.ppermute(mlp_part[chip_rows:], 'cx', swap)]
    all_gather x1 -> x0, waiting for transfers between devices: 27.3 us -> none  [body(): pair_normed = lax.all_gather(chip_normed, 'cx', axis=0, tiled=True)]
    reduce_scatter x1, waiting for transfers between devices: 31.3 us -> 12.6 us  [body(): lax.psum_scatter(mlp_chip, 'head', scatter_dimension=0, tiled=True)]
    ppermute x0 -> x2, starting transfers between devices: none -> 5.2 us  [the longest x1 3.38 us: body(): lax.ppermute(chip_normed, 'cx', swap)]
  transfers between devices with their start and end apart: 6 -> 7, of which waited for: 5 -> 6; matrix products, arithmetic and copies ran while one was open for 8% -> 8% of each run, Pallas kernels for 13% -> 13%
where the time goes in v6:
time: 262 us
  waiting for transfers between devices  163 us (62%)
  Pallas kernels  35.2 us (13%)
  other arithmetic  16.1 us (6%)
  matrix products  15.3 us (6%)
  between operations  13.3 us (5%)
  starting transfers between devices  13.2 us (5%)
  local copies, waits for them, and re-layouts  3.42 us (1%)
    all_to_all x1, waiting for transfers between devices, body(): lax.all_to_all(sums_t.astype(jnp.bfloat16), CELL + ('head',), split_axis=...  65 us
    all_gather x1, waiting for transfers between devices, body(): queries = lax.all_gather(local_queries, CELL, axis=0, tiled=True)  43.7 us
    pallas_call x1, Pallas kernels, block_attention(): pl.pallas_call(attention_kernel, grid=(pairs, lat // tile), in_specs=[pl....  35.2 us
    ppermute x1, waiting for transfers between devices, body(): lax.ppermute(mlp_part[chip_rows:], 'cx', swap)  22.9 us
    reduce_scatter x1, waiting for transfers between devices, body(): lax.psum_scatter(mlp_chip, 'head', scatter_dimension=0, tiled=True)  12.6 us
    ppermute x1, waiting for transfers between devices, body(): lax.ppermute(chip_normed, 'cx', swap)  12.3 us
    all_to_all x1, waiting for transfers between devices, body(): lax.all_to_all(ml, CELL + ('head',), split_axis=1, concat_axis=0, tiled=T...  6.43 us
    dot_general x1, matrix products, body(): mlp_part = jnp.dot(hidden, w_pack[1], preferred_element_type=jnp.float32)  6.17 us
  transfers between devices with their start and end apart: 7, of which 6 were waited for; matrix products, arithmetic and copies ran while one was open for 8% of the time, Pallas kernels for 13%

profile of v6, /device:TPU:0, one launch (start us, length us, event | category | flops | bytes accessed | tf_op | source)
XLA Modules:
  0.0 262.0 jit_solution(16133791260254195042)
XLA Ops:
  6.5 0.0 copy-start
  6.5 0.0 copy-start.4
  6.5 0.0 all-gather.3.cloned.1.call-start
  6.5 2.7 %convolution_convert_fusion.2 = bf16[256,512]{1,0:T(8,128)(2,1)} fusion(bf16[256,1024]{1,0:T(8,128)(2,1)} %param.8, bf16[1024,512]{1,0:T(8,128)(2,1)} %param.10), kind=kOutput, calls=%fused_computation.20 | convolution fusion | flops 268566528 | bytes 1835008 | tf_op jit(solution)/shard_map/dot_general | solution.py:64
  9.2 0.0 all-gather.3.cloned.1.call-update
  9.2 0.0 all-gather.5.cloned.1.call-start
  9.3 0.0 copy-done.4
  9.3 0.2 copy.30
  9.5 2.1 pad_maximum_fusion
  11.6 0.0 all-gather.5.cloned.1.call-update
  11.7 0.0 copy-done
  11.7 0.0 copy-start.5
  11.7 3.6 %convolution_convert_fusion.1.k_ref = bf16[1024,512]{1,0:T(8,128)(2,1)} fusion(bf16[1024,1024]{1,0:T(8,128)(2,1)S(1)} %copy-done, bf16[1024,512]{1,0:T(8,128)(2,1)} %param.11), kind=kOutput, calls=%fused_computation.18 | convolution fusion | flops 1074266112 | bytes 4194304 | tf_op jit(solution)/shard_map/dot_general | solution.py:62
  15.3 0.0 copy-done.5
  15.3 2.4 convolution_convert_fusion.vt_ref
  17.6 43.7 %all-gather.3.cloned.1.call-done.q_ref = bf16[2048,512]{1,0:T(8,128)(2,1)} async-done(((bf16[256,512]{1,0:T(8,128)(2,1)}), bf16[2048,512]{1,0:T(8,128)(2,1)}) %all-gather.3.cloned.1.call-update) | async-done | bytes 2097168 | tf_op jit(solution)/shard_map/all_gather | solution.py:67
  61.3 35.2 %shard_map.82 = (f32[512,2048]{1,0:T(8,128)}, f32[2,4,2,2048]{3,2,1,0:T(2,128)}) custom-call(bf16[2048,512]{1,0:T(8,128)(2,1)} %all-gather.3.cloned.1.call-done.q_ref, bf16[1024,512]{1,0:T(8,128)(2,1)} %convolution_convert_fusion.1.k_ref, bf16[512,1024]{1,0:T(8,128)(2,1)} %convolution_convert_fusion.vt_ref), custom_call_target="tpu_custom_call" | custom-call | tf_op jit(solution)/shard_map/pallas_call | solution.py:42
  96.5 1.0 all_to_all.22
  97.5 0.7 copy.23
  98.2 3.5 %all-to-all-start = ((f32[16,16,128]{2,0,1:T(8,128)}), f32[16,16,128]{2,0,1:T(8,128)S(1)}, u32[]{:S(2)}, u32[]{:S(2)}) async-start(f32[16,16,128]{2,0,1:T(8,128)} %copy.23), calls=%async_computation | async-start | bytes 262144 | tf_op jit(solution)/shard_map/all_to_all | solution.py:80
  101.8 4.0 %copy_bitcast_fusion = bf16[512,16,128]{2,0,1:T(8,128)(2,1)} fusion(f32[512,2048]{1,0:T(8,128)} %get-tuple-element.8), kind=kLoop, calls=%fused_computation.11 | loop fusion | flops 1048576 | bytes 6291456 | tf_op jit(solution)/shard_map/all_to_all | solution.py:77
  105.7 6.4 %all-to-all-done = f32[16,16,128]{2,0,1:T(8,128)S(1)} async-done(((f32[16,16,128]{2,0,1:T(8,128)}), f32[16,16,128]{2,0,1:T(8,128)S(1)}, u32[]{:S(2)}, u32[]{:S(2)}) %all-to-all-start) | async-done | bytes 131104 | tf_op jit(solution)/shard_map/all_to_all | solution.py:80
  112.2 4.4 %all-to-all-start.1 = ((bf16[512,16,128]{2,0,1:T(8,128)(2,1)}), bf16[512,16,128]{2,0,1:T(8,128)(2,1)}, u32[]{:S(2)}, u32[]{:S(2)}) async-start(bf16[512,16,128]{2,0,1:T(8,128)(2,1)} %copy_bitcast_fusion), calls=%async_computation.1 | async-start | bytes 4194304 | tf_op jit(solution)/shard_map/all_to_all | solution.py:77
  116.6 0.0 reduce-scatter.2.cloned.1.call-start
  116.7 0.1 fusion.25
  116.8 65.0 %all-to-all-done.1 = bf16[512,16,128]{2,0,1:T(8,128)(2,1)} async-done(((bf16[512,16,128]{2,0,1:T(8,128)(2,1)}), bf16[512,16,128]{2,0,1:T(8,128)(2,1)}, u32[]{:S(2)}, u32[]{:S(2)}) %all-to-all-start.1) | async-done | bytes 2097184 | tf_op jit(solution)/shard_map/all_to_all | solution.py:77
  181.8 2.0 convert_element_type.63
  183.9 0.0 copy-start.2
  183.9 0.0 copy-start.3
  183.9 4.8 %fusion = f32[2,8,64,128]{3,0,2,1:T(2,128)S(1)} fusion(f32[8,2,8,64,128]{4,3,2,1,0:T(8,128)S(1)} %bitcast.47, f32[8,2,8,128]{3,1,0,2:T(2,128)S(1)} %get-tuple-element.10), kind=kLoop, calls=%fused_computation.1 | loop fusion | flops 1966080 | bytes 4784128 | tf_op jit(solution)/shard_map/reduce_sum | solution.py:88
  188.7 0.1 fusion.23
  188.8 0.0 copy-done.2
  188.8 0.0 copy-done.3
  188.8 0.6 multiply_reduce_fusion
  189.4 0.1 multiply_convert_fusion
  189.5 2.4 all_gather.10
  191.8 3.4 %collective-permute-start = (bf16[256,1024]{1,0:T(8,128)(2,1)S(1)}, bf16[256,1024]{1,0:T(8,128)(2,1)}, u32[]{:S(2)}, u32[]{:S(2)}) collective-permute-start(bf16[256,1024]{1,0:T(8,128)(2,1)S(1)} %all_gather.10), channel_id=1, source_target_pairs={{0,2},{2,0},{1,3},{3,1},{4,6},{6,4},{5,7},{7,5},{8,10},{10,8},{9,1... | collective-permute-start | bytes 1572872 | tf_op jit(solution)/shard_map/ppermute | solution.py:106
  195.2 0.0 all-gather.5.cloned.1.call-done
  195.2 12.3 %collective-permute-done = bf16[256,1024]{1,0:T(8,128)(2,1)} collective-permute-done((bf16[256,1024]{1,0:T(8,128)(2,1)S(1)}, bf16[256,1024]{1,0:T(8,128)(2,1)}, u32[]{:S(2)}, u32[]{:S(2)}) %collective-permute-start) | collective-permute-done | bytes 524320 | tf_op jit(solution)/shard_map/ppermute | solution.py:106
  207.5 6.2 %fusion.9 = f32[512,1024]{1,0:T(8,128)} fusion(bf16[2,1024,1024]{2,1,0:T(8,128)(2,1)} %all-gather.5.cloned.1.call-done, bf16[256,1024]{1,0:T(8,128)(2,1)} %collective-permute-done, bf16[256,1024]{1,0:T(8,128)(2,1)S(1)} %all_gather.10), kind=kOutput, calls=%fused_computation.13 | convolution fusion | flops 2154299392 | bytes 7340032 | tf_op jit(solution)/shard_map/dot_general | solution.py:116
  213.7 1.5 slice.29
  215.2 1.8 collective-permute-start.1
  217.0 22.9 %collective-permute-done.1 = f32[256,1024]{1,0:T(8,128)S(1)} collective-permute-done((f32[256,1024]{1,0:T(8,128)S(1)}, f32[256,1024]{1,0:T(8,128)S(1)}, u32[]{:S(2)}, u32[]{:S(2)}) %collective-permute-start.1) | collective-permute-done | bytes 1048608 | tf_op jit(solution)/shard_map/ppermute | solution.py:118
  239.9 0.0 copy-done.1
  239.9 1.1 slice_add_fusion
  241.0 0.0 reduce-scatter.2.cloned.1.call-update
  241.0 12.6 %reduce-scatter.2.cloned.1.call-done = f32[128,1024]{1,0:T(8,128)} async-done(((f32[256,1024]{1,0:T(8,128)}), f32[128,1024]{1,0:T(8,128)}) %reduce-scatter.2.cloned.1.call-update) | async-done | bytes 524304 | tf_op jit(solution)/shard_map/reduce_scatter | solution.py:119
  253.6 1.8 add_convert_fusion
  (5 shorter events, 0.0 us)
Async XLA Ops:
  6.5 5.1 %copy-start = (bf16[1024,1024]{1,0:T(8,128)(2,1)S(1)}, bf16[1024,1024]{1,0:T(8,128)(2,1)}, u32[]{:S(2)}) copy-start(bf16[1024,1024]{1,0:T(8,128)(2,1)} %param.9) | copy-start | bytes 6291460
  6.5 2.8 %copy-start.4 = (bf16[1024,256]{1,0:T(8,128)(2,1)S(1)}, bf16[1024,256]{1,0:T(8,128)(2,1)}, u32[]{:S(2)}) copy-start(bf16[1024,256]{1,0:T(8,128)(2,1)} %param.14) | copy-start | bytes 1572868
  6.5 54.8 %all-gather.3.cloned.1.call-start = ((), (), s32[]{:S(2)}) async-start(), calls=%async_computation.3 | async-start | bytes 2359296 | tf_op jit(solution)/shard_map/all_gather | solution.py:67
  9.2 186.0 %all-gather.5.cloned.1.call-start = ((), (), s32[]{:S(2)}) async-start(), calls=%async_computation.4 | async-start | bytes 5242880 | tf_op jit(solution)/shard_map/all_gather | solution.py:103
  11.7 3.6 %copy-start.5 = (bf16[1024,512]{1,0:T(8,128)(2,1)S(1)}, bf16[1024,512]{1,0:T(8,128)(2,1)}, u32[]{:S(2)}) copy-start(bf16[1024,512]{1,0:T(8,128)(2,1)} %param.12) | copy-start | bytes 3145732
  98.2 13.9 %all-to-all-start = ((f32[16,16,128]{2,0,1:T(8,128)}), f32[16,16,128]{2,0,1:T(8,128)S(1)}, u32[]{:S(2)}, u32[]{:S(2)}) async-start(f32[16,16,128]{2,0,1:T(8,128)} %copy.23), calls=%async_computation | async-start | bytes 262144 | tf_op jit(solution)/shard_map/all_to_all | solution.py:80
  112.2 69.7 %all-to-all-start.1 = ((bf16[512,16,128]{2,0,1:T(8,128)(2,1)}), bf16[512,16,128]{2,0,1:T(8,128)(2,1)}, u32[]{:S(2)}, u32[]{:S(2)}) async-start(bf16[512,16,128]{2,0,1:T(8,128)(2,1)} %copy_bitcast_fusion), calls=%async_computation.1 | async-start | bytes 4194304 | tf_op jit(solution)/shard_map/all_to_all | solution.py:77
  116.6 137.0 %reduce-scatter.2.cloned.1.call-start = ((), (), s32[]{:S(2)}) async-start(), calls=%async_computation.5 | async-start | bytes 1572864 | tf_op jit(solution)/shard_map/reduce_scatter | solution.py:119
  183.9 4.9 %copy-start.2 = (bf16[1024,1024]{1,0:T(8,128)(2,1)S(1)}, bf16[1024,1024]{1,0:T(8,128)(2,1)}, u32[]{:S(2)}) copy-start(bf16[1024,1024]{1,0:T(8,128)(2,1)} %param.13) | copy-start | bytes 6291460
  183.9 4.9 %copy-start.3 = (bf16[256,1024]{1,0:T(8,128)(2,1)S(1)}, bf16[256,1024]{1,0:T(8,128)(2,1)}, u32[]{:S(2)}) copy-start(bf16[256,1024]{1,0:T(8,128)(2,1)} %param.8) | copy-start | bytes 1572868
  191.8 15.7 %collective-permute-start = (bf16[256,1024]{1,0:T(8,128)(2,1)S(1)}, bf16[256,1024]{1,0:T(8,128)(2,1)}, u32[]{:S(2)}, u32[]{:S(2)}) collective-permute-start(bf16[256,1024]{1,0:T(8,128)(2,1)S(1)} %all_gather.10), channel_id=1, source_target_pairs={{0,2},{2,0},{1,3},{3,1},{4,6},{6,4},{5,7},{7,5},{8,10},{10,8},{9,1... | collective-permute-start | bytes 1572872 | tf_op jit(solution)/shard_map/ppermute | solution.py:106
  213.7 26.2 %copy-start.1 = (f32[512,1024]{1,0:T(8,128)S(1)}, f32[512,1024]{1,0:T(8,128)}, u32[]{:S(2)}) copy-start(f32[512,1024]{1,0:T(8,128)} %fusion.9) | copy-start | bytes 6291460
  215.2 24.7 %collective-permute-start.1 = (f32[256,1024]{1,0:T(8,128)S(1)}, f32[256,1024]{1,0:T(8,128)S(1)}, u32[]{:S(2)}, u32[]{:S(2)}) collective-permute-start(f32[256,1024]{1,0:T(8,128)S(1)} %slice.29), channel_id=1, source_target_pairs={{0,2},{2,0},{1,3},{3,1},{4,6},{6,4},{5,7},{7,5},{8,10},{10,8},{9,1... | collective-permute-start | bytes 3145736 | tf_op jit(solution)/shard_map/ppermute | solution.py:118
Sparse Core Ops, SparseCore 0:
  9.5 51.7 all-gather.2
  62.9 117.1 all-gather.4
  241.1 12.4 reduce-scatter.1

commit v7 on v6

--- a/solution.py
+++ b/solution.py
@@ -64,19 +64,28 @@
     local_queries = jnp.dot(latents, w_query, preferred_element_type=jnp.float32).astype(
         jnp.bfloat16
     )
-    queries = lax.all_gather(local_queries, CELL, axis=0, tiled=True)
     n_cell = lax.axis_size(CELL)
-    lat, width = queries.shape
+    n_head = lax.axis_size("head")
+    lat = n_cell * local_queries.shape[0]
+    width = local_queries.shape[1]
     heads_local = width // HEAD_DIM
-    n_head = lax.axis_size("head")
     owners = n_cell * n_head
     rows = lat // owners
-
-    sums_t, ml = block_attention(queries, key_rows, value_t)
-    ml = ml.reshape(2 * heads_local, lat)
-    sums_recv = lax.all_to_all(
-        sums_t.astype(jnp.bfloat16), CELL + ("head",), split_axis=1, concat_axis=0, tiled=True
-    )
+    half = width // 2
+    sums_parts = []
+    ml_parts = []
+    for part in range(2):
+        cols = slice(part * half, (part + 1) * half)
+        queries = lax.all_gather(local_queries[:, cols], CELL, axis=0, tiled=True)
+        sums_t, ml = block_attention(queries, key_rows[:, cols], value_t[cols])
+        sums_parts.append(
+            lax.all_to_all(
+                sums_t.astype(jnp.bfloat16), CELL + ("head",), split_axis=1, concat_axis=0, tiled=True
+            ).reshape(owners, half, rows)
+        )
+        ml_parts.append(ml.reshape(2, heads_local // 2, lat))
+    ml = jnp.concatenate(ml_parts, axis=1).reshape(2 * heads_local, lat)
+    sums_recv = jnp.concatenate(sums_parts, axis=1)
     ml_recv = lax.all_to_all(ml, CELL + ("head",), split_axis=1, concat_axis=0, tiled=True)
     sums_recv = sums_recv.reshape(n_cell, n_head, heads_local, HEAD_DIM, rows).astype(jnp.float32)
     ml_recv = ml_recv.reshape(n_cell, n_head, 2, heads_local, rows)
@@ -115,7 +124,8 @@
     ).astype(jnp.bfloat16)
     mlp_part = jnp.dot(hidden, w_pack[1], preferred_element_type=jnp.float32)
     chip_rows = chip_normed.shape[0]
-    mlp_chip = mlp_part[:chip_rows] + lax.ppermute(mlp_part[chip_rows:], "cx", swap)
+    back = lax.ppermute(mlp_part[chip_rows:].astype(jnp.bfloat16), "cx", swap)
+    mlp_chip = mlp_part[:chip_rows] + back.astype(jnp.float32)
     mlp_out = lax.psum_scatter(mlp_chip, "head", scatter_dimension=0, tiled=True)
     return (widened + mlp_out).astype(jnp.bfloat16)
 

time: 262 us -> 285 us (1.088)
  starting transfers between devices: 13.2 us -> 32.7 us
  local copies, waits for them, and re-layouts: 3.42 us -> 7.42 us
  waiting for transfers between devices: 163 us -> 160 us
    all_to_all x1 -> x2, starting transfers between devices: 4.43 us -> 25.1 us  [body(): lax.all_to_all(sums_t.astype(jnp.bfloat16), CELL + ('head',), split_axis=...]
    all_gather x1 -> x2, waiting for transfers between devices: 43.7 us -> 55.3 us  [body(): queries = lax.all_gather(local_queries[:, cols], CELL, axis=0, tiled=True)]
    ppermute x1, waiting for transfers between devices: 22.9 us -> 11.6 us  [body(): back = lax.ppermute(mlp_part[chip_rows:].astype(jnp.bfloat16), 'cx', swap)]
    reduce_scatter x1, waiting for transfers between devices: 12.6 us -> 9.67 us  [body(): lax.psum_scatter(mlp_chip, 'head', scatter_dimension=0, tiled=True)]
    all_to_all x1 -> x2, waiting for transfers between devices: 65 us -> 62.6 us  [body(): lax.all_to_all(sums_t.astype(jnp.bfloat16), CELL + ('head',), split_axis=...]
    pallas_call x1 -> x2, Pallas kernels: 35.2 us -> 37 us  [block_attention(): pl.pallas_call(attention_kernel, grid=(pairs, lat // tile), in_specs=[pl....]
  transfers between devices with their start and end apart: 7 -> 9, of which waited for: 6 -> 8; matrix products, arithmetic and copies ran while one was open for 8% -> 8% of each run, Pallas kernels for 13% -> 13%
where the time goes in v7:
time: 285 us; the launch traced here: 284 us
  waiting for transfers between devices  160 us (56%)
  Pallas kernels  37 us (13%)
  starting transfers between devices  32.7 us (11%)
  other arithmetic  18.9 us (7%)
  between operations  13.4 us (5%)
  matrix products  12.5 us (4%)
  local copies, waits for them, and re-layouts  7.42 us (3%)
    all_to_all x2, waiting for transfers between devices, body(): lax.all_to_all(sums_t.astype(jnp.bfloat16), CELL + ('head',), split_axis=...  62.6 us
    all_gather x2, waiting for transfers between devices, body(): queries = lax.all_gather(local_queries[:, cols], CELL, axis=0, tiled=True)  55.3 us
    pallas_call x2, Pallas kernels, block_attention(): pl.pallas_call(attention_kernel, grid=(pairs, lat // tile), in_specs=[pl....  37 us
    all_to_all x2, starting transfers between devices, body(): lax.all_to_all(sums_t.astype(jnp.bfloat16), CELL + ('head',), split_axis=...  25.1 us
    ppermute x1, waiting for transfers between devices, body(): lax.ppermute(chip_normed, 'cx', swap)  12.3 us
    ppermute x1, waiting for transfers between devices, body(): back = lax.ppermute(mlp_part[chip_rows:].astype(jnp.bfloat16), 'cx', swap)  11.6 us
    reduce_scatter x1, waiting for transfers between devices, body(): lax.psum_scatter(mlp_chip, 'head', scatter_dimension=0, tiled=True)  9.67 us
    all_to_all x1, waiting for transfers between devices, body(): lax.all_to_all(ml, CELL + ('head',), split_axis=1, concat_axis=0, tiled=T...  7.61 us
  transfers between devices with their start and end apart: 9, of which 8 were waited for; matrix products, arithmetic and copies ran while one was open for 8% of the time, Pallas kernels for 13%

profile of v7, /device:TPU:0, one launch (start us, length us, event | category | flops | bytes accessed | tf_op | source)
XLA Modules:
  0.0 283.9 jit_solution(18415196135345358971)
XLA Ops:
  6.5 2.0 convolution_convert_fusion.2
  8.5 0.7 fusion.37
  9.2 0.0 all-gather.4.cloned.1.call-update
  9.3 0.0 all-gather.6.cloned.1.call-start
  9.3 0.7 all-gather.6.cloned.1.call-update
  10.0 0.0 all-gather.8.cloned.1.call-start
  10.1 0.2 copy.32
  10.3 2.2 pad_maximum_fusion.1
  12.5 0.0 all-gather.8.cloned.1.call-update
  12.5 2.5 convolution_convert_fusion
  15.0 1.0 fusion.35
  16.1 0.6 copy-done.4
  16.6 1.2 convolution_convert_fusion.1
  17.9 1.1 fusion.36
  19.0 33.5 %all-gather.4.cloned.1.call-done.q_ref = bf16[2048,256]{1,0:T(8,128)(2,1)} async-done(((bf16[256,256]{1,0:T(8,128)(2,1)}), bf16[2048,256]{1,0:T(8,128)(2,1)}) %all-gather.4.cloned.1.call-update) | async-done | bytes 1048592 | tf_op jit(solution)/shard_map/all_gather | solution.py:79
  52.5 18.5 %shard_map.82 = (f32[256,2048]{1,0:T(8,128)}, f32[2,2,2,2048]{3,2,1,0:T(2,128)}) custom-call(bf16[2048,256]{1,0:T(8,128)(2,1)} %all-gather.4.cloned.1.call-done.q_ref, bf16[1024,256]{1,0:T(8,128)(2,1)} %get-tuple-element.17.k_ref, bf16[256,1024]{1,0:T(8,128)(2,1)} %get-tuple-element.15.vt_ref), custom_call_target="tpu_custom_call" | custom-call | tf_op jit(solution)/shard_map/pallas_call | solution.py:42
  71.0 0.9 reshape.49
  71.9 21.8 %all-gather.6.cloned.1.call-done.q_ref = bf16[2048,256]{1,0:T(8,128)(2,1)} async-done(((bf16[256,256]{1,0:T(8,128)(2,1)}), bf16[2048,256]{1,0:T(8,128)(2,1)}) %all-gather.6.cloned.1.call-update) | async-done | bytes 1048592 | tf_op jit(solution)/shard_map/all_gather | solution.py:79
  93.7 18.5 %shard_map.83 = (f32[256,2048]{1,0:T(8,128)}, f32[2,2,2,2048]{3,2,1,0:T(2,128)}) custom-call(bf16[2048,256]{1,0:T(8,128)(2,1)} %all-gather.6.cloned.1.call-done.q_ref, bf16[1024,256]{1,0:T(8,128)(2,1)} %get-tuple-element.18.k_ref, bf16[256,1024]{1,0:T(8,128)(2,1)} %get-tuple-element.16.vt_ref), custom_call_target="tpu_custom_call" | custom-call | tf_op jit(solution)/shard_map/pallas_call | solution.py:42
  112.2 0.9 reshape.50
  113.1 0.7 copy.24
  113.8 3.5 %all-to-all-start = ((f32[16,16,128]{2,0,1:T(8,128)}), f32[16,16,128]{2,0,1:T(8,128)S(1)}, u32[]{:S(2)}, u32[]{:S(2)}) async-start(f32[16,16,128]{2,0,1:T(8,128)} %copy.24), calls=%async_computation | async-start | bytes 262144 | tf_op jit(solution)/shard_map/all_to_all | solution.py:89
  117.4 2.8 copy_bitcast_fusion.1
  120.2 7.6 %all-to-all-done = f32[16,16,128]{2,0,1:T(8,128)S(1)} async-done(((f32[16,16,128]{2,0,1:T(8,128)}), f32[16,16,128]{2,0,1:T(8,128)S(1)}, u32[]{:S(2)}, u32[]{:S(2)}) %all-to-all-start) | async-done | bytes 131104 | tf_op jit(solution)/shard_map/all_to_all | solution.py:89
  127.8 4.2 %all-to-all-start.1 = ((bf16[256,16,128]{2,0,1:T(8,128)(2,1)}), bf16[256,16,128]{2,0,1:T(8,128)(2,1)S(1)}, u32[]{:S(2)}, u32[]{:S(2)}) async-start(bf16[256,16,128]{2,0,1:T(8,128)(2,1)} %copy_bitcast_fusion.1), calls=%async_computation.1 | async-start | bytes 2097152 | tf_op jit(solution)/shard_map/all_to_all | solution.py:82
  132.0 2.8 copy_bitcast_fusion
  134.8 37.1 %all-to-all-done.1 = bf16[256,16,128]{2,0,1:T(8,128)(2,1)S(1)} async-done(((bf16[256,16,128]{2,0,1:T(8,128)(2,1)}), bf16[256,16,128]{2,0,1:T(8,128)(2,1)S(1)}, u32[]{:S(2)}, u32[]{:S(2)}) %all-to-all-start.1) | async-done | bytes 1048608 | tf_op jit(solution)/shard_map/all_to_all | solution.py:82
  171.9 20.8 %all-to-all-start.2 = ((bf16[256,16,128]{2,0,1:T(8,128)(2,1)}), bf16[256,16,128]{2,0,1:T(8,128)(2,1)}, u32[]{:S(2)}, u32[]{:S(2)}) async-start(bf16[256,16,128]{2,0,1:T(8,128)(2,1)} %copy_bitcast_fusion), calls=%async_computation.2 | async-start | bytes 2097152 | tf_op jit(solution)/shard_map/all_to_all | solution.py:82
  192.8 0.2 reduce-scatter.2.cloned.1.call-start
  193.1 0.1 fusion.25
  193.2 25.4 %all-to-all-done.2 = bf16[256,16,128]{2,0,1:T(8,128)(2,1)} async-done(((bf16[256,16,128]{2,0,1:T(8,128)(2,1)}), bf16[256,16,128]{2,0,1:T(8,128)(2,1)}, u32[]{:S(2)}, u32[]{:S(2)}) %all-to-all-start.2) | async-done | bytes 1048608 | tf_op jit(solution)/shard_map/all_to_all | solution.py:82
  218.6 1.4 pad_maximum_fusion
  220.0 0.5 convert.5
  220.5 4.8 %fusion = f32[2,8,64,128]{3,0,2,1:T(2,128)S(1)} fusion(f32[8,2,8,64,128]{4,3,2,1,0:T(8,128)S(1)} %convert.5, f32[8,2,8,128]{3,1,0,2:T(2,128)S(1)} %get-tuple-element.14), kind=kLoop, calls=%fused_computation.1 | loop fusion | flops 1966080 | bytes 4784128 | tf_op jit(solution)/shard_map/reduce_sum | solution.py:97
  225.3 0.1 fusion.23
  225.4 0.6 multiply_reduce_fusion
  226.0 0.1 multiply_convert_fusion
  226.1 2.2 all_gather.14
  228.3 2.0 collective-permute-start
  230.2 12.3 %collective-permute-done = bf16[256,1024]{1,0:T(8,128)(2,1)} collective-permute-done((bf16[256,1024]{1,0:T(8,128)(2,1)S(1)}, bf16[256,1024]{1,0:T(8,128)(2,1)}, u32[]{:S(2)}, u32[]{:S(2)}) %collective-permute-start) | collective-permute-done | bytes 524320 | tf_op jit(solution)/shard_map/ppermute | solution.py:115
  242.6 6.2 %fusion.9 = f32[512,1024]{1,0:T(8,128)} fusion(bf16[2,1024,1024]{2,1,0:T(8,128)(2,1)} %all-gather.8.cloned.1.call-done, bf16[256,1024]{1,0:T(8,128)(2,1)} %collective-permute-done, bf16[256,1024]{1,0:T(8,128)(2,1)S(1)} %all_gather.14), kind=kOutput, calls=%fused_computation.12 | convolution fusion | flops 2154299392 | bytes 7340032 | tf_op jit(solution)/shard_map/dot_general | solution.py:125
  248.8 1.3 slice.72
  250.1 1.8 collective-permute-start.1
  251.9 11.6 %collective-permute-done.1 = bf16[256,1024]{1,0:T(8,128)(2,1)S(1)} collective-permute-done((bf16[256,1024]{1,0:T(8,128)(2,1)S(1)}, bf16[256,1024]{1,0:T(8,128)(2,1)S(1)}, u32[]{:S(2)}, u32[]{:S(2)}) %collective-permute-start.1) | collective-permute-done | bytes 524320 | tf_op jit(solution)/shard_map/ppermute | solution.py:127
  263.5 2.4 slice_add_fusion
  265.9 0.0 reduce-scatter.2.cloned.1.call-update
  265.9 9.7 %reduce-scatter.2.cloned.1.call-done = f32[128,1024]{1,0:T(8,128)} async-done(((f32[256,1024]{1,0:T(8,128)}), f32[128,1024]{1,0:T(8,128)}) %reduce-scatter.2.cloned.1.call-update) | async-done | bytes 524304 | tf_op jit(solution)/shard_map/reduce_scatter | solution.py:129
  275.6 1.8 add_convert_fusion
  (17 shorter events, 0.1 us)
Async XLA Ops:
  6.5 6.0 %copy-start = (bf16[1024,1024]{1,0:T(8,128)(2,1)S(1)}, bf16[1024,1024]{1,0:T(8,128)(2,1)}, u32[]{:S(2)}) copy-start(bf16[1024,1024]{1,0:T(8,128)(2,1)} %param.9) | copy-start | bytes 6291460
  6.5 3.5 %copy-start.3 = (bf16[1024,256]{1,0:T(8,128)(2,1)S(1)}, bf16[1024,256]{1,0:T(8,128)(2,1)}, u32[]{:S(2)}) copy-start(bf16[1024,256]{1,0:T(8,128)(2,1)} %param.14) | copy-start | bytes 1572868
  6.5 46.0 %all-gather.4.cloned.1.call-start = ((), (), s32[]{:S(2)}) async-start(), calls=%async_computation.4 | async-start | bytes 1179648 | tf_op jit(solution)/shard_map/all_gather | solution.py:79
  9.3 84.4 %all-gather.6.cloned.1.call-start = ((), (), s32[]{:S(2)}) async-start(), calls=%async_computation.5 | async-start | bytes 1179648 | tf_op jit(solution)/shard_map/all_gather | solution.py:79
  10.0 232.6 %all-gather.8.cloned.1.call-start = ((), (), s32[]{:S(2)}) async-start(), calls=%async_computation.6 | async-start | bytes 5242880 | tf_op jit(solution)/shard_map/all_gather | solution.py:112
  15.0 1.6 copy-start.4
  113.8 13.9 %all-to-all-start = ((f32[16,16,128]{2,0,1:T(8,128)}), f32[16,16,128]{2,0,1:T(8,128)S(1)}, u32[]{:S(2)}, u32[]{:S(2)}) async-start(f32[16,16,128]{2,0,1:T(8,128)} %copy.24), calls=%async_computation | async-start | bytes 262144 | tf_op jit(solution)/shard_map/all_to_all | solution.py:89
  127.8 44.2 %all-to-all-start.1 = ((bf16[256,16,128]{2,0,1:T(8,128)(2,1)}), bf16[256,16,128]{2,0,1:T(8,128)(2,1)S(1)}, u32[]{:S(2)}, u32[]{:S(2)}) async-start(bf16[256,16,128]{2,0,1:T(8,128)(2,1)} %copy_bitcast_fusion.1), calls=%async_computation.1 | async-start | bytes 2097152 | tf_op jit(solution)/shard_map/all_to_all | solution.py:82
  171.9 46.7 %all-to-all-start.2 = ((bf16[256,16,128]{2,0,1:T(8,128)(2,1)}), bf16[256,16,128]{2,0,1:T(8,128)(2,1)}, u32[]{:S(2)}, u32[]{:S(2)}) async-start(bf16[256,16,128]{2,0,1:T(8,128)(2,1)} %copy_bitcast_fusion), calls=%async_computation.2 | async-start | bytes 2097152 | tf_op jit(solution)/shard_map/all_to_all | solution.py:82
  192.8 82.8 %reduce-scatter.2.cloned.1.call-start = ((), (), s32[]{:S(2)}) async-start(), calls=%async_computation.7 | async-start | bytes 1572864 | tf_op jit(solution)/shard_map/reduce_scatter | solution.py:129
  220.5 4.9 %copy-start.1 = (bf16[1024,1024]{1,0:T(8,128)(2,1)S(1)}, bf16[1024,1024]{1,0:T(8,128)(2,1)}, u32[]{:S(2)}) copy-start(bf16[1024,1024]{1,0:T(8,128)(2,1)} %param.13) | copy-start | bytes 6291460
  220.5 4.9 %copy-start.2 = (bf16[256,1024]{1,0:T(8,128)(2,1)S(1)}, bf16[256,1024]{1,0:T(8,128)(2,1)}, u32[]{:S(2)}) copy-start(bf16[256,1024]{1,0:T(8,128)(2,1)} %param.8) | copy-start | bytes 1572868
  228.3 14.3 %collective-permute-start = (bf16[256,1024]{1,0:T(8,128)(2,1)S(1)}, bf16[256,1024]{1,0:T(8,128)(2,1)}, u32[]{:S(2)}, u32[]{:S(2)}) collective-permute-start(bf16[256,1024]{1,0:T(8,128)(2,1)S(1)} %all_gather.14), channel_id=1, source_target_pairs={{0,2},{2,0},{1,3},{3,1},{4,6},{6,4},{5,7},{7,5},{8,10},{10,8},{9,1... | collective-permute-start | bytes 1572872 | tf_op jit(solution)/shard_map/ppermute | solution.py:115
  250.1 13.4 %collective-permute-start.1 = (bf16[256,1024]{1,0:T(8,128)(2,1)S(1)}, bf16[256,1024]{1,0:T(8,128)(2,1)S(1)}, u32[]{:S(2)}, u32[]{:S(2)}) collective-permute-start(bf16[256,1024]{1,0:T(8,128)(2,1)S(1)} %slice.72), channel_id=1, source_target_pairs={{0,2},{2,0},{1,3},{3,1},{4,6},{6,4},{5,7},{7,5},{8,10},{10,8},{9,1... | collective-permute-start | bytes 1572872 | tf_op jit(solution)/shard_map/ppermute | solution.py:127
Sparse Core Ops, SparseCore 0:
  9.5 42.9 all-gather.3
  54.6 39.0 all-gather.5
  95.2 118.4 all-gather.7
  266.0 9.5 reduce-scatter.1
